TPU v7x, 128 devices: a whole 4x4x4 slice. The times are simulated.
128 devices in a mesh: dp: 8 (over x_hi, z), tensor: 16 (over y, x_lo, core).
Axes of the slice: x: 4 (x_hi: 2, x_lo: 2; x = x_hi * 2 + x_lo), y: 4, z: 4, core: 2. Of those that a mesh axis runs over, the one named last changes fastest.
Arguments:
- tokens: bfloat16 [16384, 2048], P(('dp', 'tensor')), parts along dimension 0, may hold values from -6 to 6
- segment_ids: int32 [16384], P('dp'), parts along dimension 0, may hold values from 0 to 3, never falling along the last dimension, each value on 1 to 1024 neighbouring positions
- attention_gain: float32 [2048], replicated, may hold values from 0.1 to 1.9
- query_weight: bfloat16 [2048, 2048], P(None, 'tensor'), may hold values from -1 to 1
- key_weight: bfloat16 [2048, 2048], P(None, 'tensor'), may hold values from -1 to 1
- value_weight: bfloat16 [2048, 2048], P(None, 'tensor'), may hold values from -0.125 to 0.125
- output_weight: bfloat16 [2048, 2048], P('tensor'), may hold values from -0.125 to 0.125
- ffn_gain: float32 [2048], replicated, may hold values from 0.1 to 1.9
- shared_gate: bfloat16 [2048, 2816], P(None, 'tensor'), may hold values from -0.125 to 0.125
- shared_up: bfloat16 [2048, 2816], P(None, 'tensor'), may hold values from -0.125 to 0.125
- shared_down: bfloat16 [2816, 2048], P('tensor'), may hold values from -0.109375 to 0.109375
- expert_gate: bfloat16 [16, 2048, 1408], P('tensor'), may hold values from -0.125 to 0.125
- expert_up: bfloat16 [16, 2048, 1408], P('tensor'), may hold values from -0.125 to 0.125
- expert_down: bfloat16 [16, 1408, 2048], P('tensor'), may hold values from -0.15625 to 0.15625
- expert_ids: int32 [16384, 6], P('dp'), parts along dimension 0, may hold values from 0 to 15, all different within a row; in each aligned block of 128 rows (0 to 127, 128 to 255, ...) at most 64 rows name the same one
- gate_weights: float32 [16384, 6], P('dp'), parts along dimension 0, may hold values from 0.05 to 0.35
- page_table: int32 [128], P('dp'), parts along dimension 0, may hold values from 0 to 15, each once
Outputs:
- layer_out: bfloat16 [16384, 2048], P(('dp', 'tensor')), parts along dimension 0
- kv_pages: bfloat16 [2, 128, 128, 2048], P(None, 'dp', None, 'tensor'), parts along dimension 1
There are 8 independent parts, one for each index of `dp`. A program takes and returns all parts, laid end to end along the dimension named above; an argument that names none is the same for every part. Nothing has to cross between parts.
Inputs may be any that keep to these rules, and one draw needn't show every extreme that they name: `segment_ids`: ids never fall along the stream; each of the 4 prompts holds 1 to 1024 tokens and one holds exactly 1024. `expert_ids`: each row names 6 different experts; within each aligned block of 128 rows (the tokens of one index of tensor) no expert is named by more than 64 rows, a bound that some block reaches. `page_table`: each cache page is named once.
All inputs are finite; a program needn't handle non-finite values.
Results may differ from a plain program's by a relative error of at most 0.02.
The roundings to bfloat16 on the way count: a program that leaves them out, or rounds other values in their place, can miss the bound.
Values may be sent and summed in bfloat16 or wider, within the bound.
No kernel may reach another device: no remote copies, remote signals or barrier semaphores. Data moves between devices by JAX's collectives and lax.ppermute only.
A program may use at most 128 MiB of HBM per device.

v0:
```python
import jax
import jax.numpy as jnp
from jax import lax
from jax.sharding import PartitionSpec as P

HD = 128
TOP = 6
PAGE = 128


def rms_scale(hidden, gain):
    widened = hidden.astype(jnp.float32)
    inverse = lax.rsqrt(jnp.mean(widened * widened, axis=-1, keepdims=True) + 1e-06)
    return (widened * inverse * gain).astype(jnp.bfloat16)


def attend(projected, segment_ids, head_count):
    total_tokens = projected.shape[0]
    inner = head_count * HD
    queries = projected[:, :inner].reshape(total_tokens, head_count, HD)
    keys = projected[:, inner : 2 * inner].reshape(total_tokens, head_count, HD)
    values = projected[:, 2 * inner :].reshape(total_tokens, head_count, HD)
    scale = HD ** (-0.5)
    positions = jnp.arange(total_tokens, dtype=jnp.int32)
    span = min(512, total_tokens)

    def one_block(start):
        query_rows = lax.dynamic_slice_in_dim(queries, start, span, 0)
        query_segments = lax.dynamic_slice_in_dim(segment_ids, start, span, 0)
        query_positions = start + jnp.arange(span, dtype=jnp.int32)
        scores = (
            jnp.einsum("qhd,khd->hqk", query_rows, keys, preferred_element_type=jnp.float32) * scale
        )
        allowed = (query_segments[:, None] == segment_ids[None, :]) & (
            positions[None, :] <= query_positions[:, None]
        )
        scores = jnp.where(allowed[None], scores, -jnp.inf)
        highest = jnp.max(scores, axis=-1, keepdims=True)
        weights = jnp.exp(scores - highest)
        probs = (weights / jnp.sum(weights, axis=-1, keepdims=True)).astype(jnp.bfloat16)
        context = jnp.einsum("hqk,khd->qhd", probs, values, preferred_element_type=jnp.float32)
        return context.astype(jnp.bfloat16)

    starts = jnp.arange(total_tokens // span, dtype=jnp.int32) * span
    context = lax.map(one_block, starts).reshape(total_tokens, inner)
    return (context, keys.reshape(total_tokens, inner), values.reshape(total_tokens, inner))


def slot_tables(block_ids, block_gates, expert_count, capacity):
    row_count = block_ids.shape[0]
    labels = jnp.arange(expert_count, dtype=jnp.int32)
    match = (block_ids[:, :, None] == labels[None, None, :]).astype(jnp.int32)
    hits = jnp.sum(match, axis=1)
    before = jnp.cumsum(hits, axis=0) - hits
    rank = jnp.sum(match * before[:, None, :], axis=2)
    flat = (block_ids * capacity + rank).reshape(-1)
    owner = jnp.broadcast_to(jnp.arange(row_count, dtype=jnp.int32)[:, None], block_ids.shape)
    slot_token = jnp.zeros((expert_count * capacity,), jnp.int32).at[flat].set(owner.reshape(-1))
    slot_weight = (
        jnp.zeros((expert_count * capacity,), jnp.float32).at[flat].set(block_gates.reshape(-1))
    )
    return (slot_token, slot_weight)


def expert_apply(incoming, expert_gate, expert_up, expert_down):
    gate_part = jnp.einsum(
        "secd,edf->secf", incoming, expert_gate, preferred_element_type=jnp.float32
    )
    upward = jnp.einsum("secd,edf->secf", incoming, expert_up, preferred_element_type=jnp.float32)
    hidden = (jax.nn.silu(gate_part) * upward).astype(jnp.bfloat16)
    produced = jnp.einsum("secf,efd->secd", hidden, expert_down, preferred_element_type=jnp.float32)
    return produced.astype(jnp.bfloat16)


def shards(
    tokens,
    segment_ids,
    attention_gain,
    query_weight,
    key_weight,
    value_weight,
    output_weight,
    ffn_gain,
    shared_gate,
    shared_up,
    shared_down,
    expert_gate,
    expert_up,
    expert_down,
    expert_ids,
    gate_weights,
    page_table,
):
    tok_dev = tokens.shape[0]
    groups = lax.axis_size("tensor")
    position = lax.axis_index("tensor")
    inner = query_weight.shape[1]
    head_count = inner // HD
    projection = jnp.concatenate([query_weight, key_weight, value_weight], axis=1)
    projected = jnp.dot(
        rms_scale(lax.all_gather(tokens, "tensor", axis=0, tiled=True), attention_gain),
        projection,
        preferred_element_type=jnp.float32,
    ).astype(jnp.bfloat16)
    context, keys, values = attend(projected, segment_ids, head_count)
    cache = jnp.stack([keys, values]).reshape(2, -1, PAGE, inner)
    kv_pages = jnp.zeros_like(cache).at[:, page_table].set(cache)
    attention = lax.psum_scatter(
        jnp.dot(context, output_weight, preferred_element_type=jnp.float32).astype(jnp.bfloat16),
        "tensor",
        scatter_dimension=0,
        tiled=True,
    ).astype(jnp.float32)
    residual = (tokens.astype(jnp.float32) + attention).astype(jnp.bfloat16)
    normed_ffn = rms_scale(residual, ffn_gain)
    shared_columns = jnp.concatenate([shared_gate, shared_up], axis=1)
    shared_width = shared_gate.shape[1]
    local_experts = expert_gate.shape[0]
    expert_count = local_experts * groups
    capacity = tok_dev * TOP // expert_count + tok_dev // 8
    id_blocks = expert_ids.reshape(groups, tok_dev, -1)
    gate_blocks = gate_weights.reshape(groups, tok_dev, -1)

    def block_table(id_block, gate_block):
        return slot_tables(id_block, gate_block, expert_count, capacity)

    all_tokens, all_weights = jax.vmap(block_table)(id_blocks, gate_blocks)
    all_tokens = all_tokens.reshape(groups, expert_count, capacity)
    all_weights = all_weights.reshape(groups, expert_count, capacity)
    chosen_slots = lax.dynamic_slice_in_dim(all_tokens, position * local_experts, local_experts, 1)
    chosen_weights = lax.dynamic_slice_in_dim(
        all_weights, position * local_experts, local_experts, 1
    )
    offsets = (jnp.arange(groups, dtype=jnp.int32) * tok_dev)[:, None, None]
    stream_slots = (chosen_slots + offsets).reshape(-1)
    joined = jnp.dot(
        lax.all_gather(normed_ffn, "tensor", axis=0, tiled=True),
        shared_columns,
        preferred_element_type=jnp.float32,
    )
    hidden_all = (jax.nn.silu(joined[:, :shared_width]) * joined[:, shared_width:]).astype(
        jnp.bfloat16
    )
    own_slots = all_tokens[position]
    outgoing = normed_ffn[own_slots.reshape(-1)].reshape(groups, local_experts, capacity, -1)
    produced = expert_apply(
        lax.all_to_all(outgoing, "tensor", split_axis=0, concat_axis=0, tiled=True),
        expert_gate,
        expert_up,
        expert_down,
    )
    term = jnp.dot(hidden_all, shared_down, preferred_element_type=jnp.float32)
    model_width = term.shape[1]
    weighted = chosen_weights.reshape(-1, 1) * produced.reshape(-1, model_width).astype(jnp.float32)
    term = term.at[stream_slots].add(weighted)
    ffn_out = lax.psum_scatter(
        term.astype(jnp.bfloat16), "tensor", scatter_dimension=0, tiled=True
    ).astype(jnp.float32)
    layer_out = (residual.astype(jnp.float32) + ffn_out).astype(jnp.bfloat16)
    return (layer_out, kv_pages)


def solution(mesh):
    placed = (
        P(("dp", "tensor"), None),
        P("dp"),
        P(),
        P(None, "tensor"),
        P(None, "tensor"),
        P(None, "tensor"),
        P("tensor", None),
        P(),
        P(None, "tensor"),
        P(None, "tensor"),
        P("tensor", None),
        P("tensor", None, None),
        P("tensor", None, None),
        P("tensor", None, None),
        P("dp", None),
        P("dp", None),
        P("dp"),
    )
    return jax.shard_map(
        shards,
        mesh=mesh,
        in_specs=placed,
        out_specs=(P(("dp", "tensor"), None), P(None, "dp", None, "tensor")),
        check_vma=False,
    )
```

profile of v0, /device:TPU:0, one launch (start us, length us, event | category | flops | bytes accessed | tf_op | source)
XLA Modules:
  0.0 538.0 jit_solution(10992776695320439391)
XLA Ops:
  7.2 0.7 all-gather.3.cloned.1.call-update
  8.0 56.3 %all-gather.3.cloned.1.call-done = bf16[2048,2048]{1,0:T(8,128)(2,1)} async-done(((bf16[128,2048]{1,0:T(8,128)(2,1)}), bf16[2048,2048]{1,0:T(8,128)(2,1)}) %all-gather.3.cloned.1.call-update) | async-done | bytes 8388624 | tf_op jit(solution)/shard_map/all_gather | solution.py:101
  64.3 5.2 fusion.13
  69.6 0.5 copy-done.2
  70.1 6.0 %fusion.44 = bf16[2048,384]{1,0:T(8,128)(2,1)S(1)} fusion(bf16[2048,2048]{1,0:T(8,128)(2,1)S(1)} %copy-done.2, f32[2048]{0:T(1024)S(1)} %copy-done.13, f32[2048]{0:T(1024)S(1)} %add_rsqrt_fusion, bf16[2048,128]{1,0:T(8,128)(2,1)S(1)} %copy-done.12, bf16[2048,128]{1,0:T(8,128)(2,1)} %param.23, bf16[2048,128]{1,0:T(8,128)(2,1)} %param.22), kind=kOutput, calls=%fused_computation.51 | convolution fusion | flops 3243507712 | bytes 11550720 | tf_op jit(solution)/shard_map/dot_general | solution.py:100
  76.1 1.2 fusion.77
  77.3 25.8 %while.11 = (s32[]{:T(128)}, bf16[4,512,1,128]{3,1,2,0:T(8,128)(2,1)S(1)}, s32[4]{0:T(128)S(1)}, s32[2048]{0:T(1024)S(1)}, bf16[2048,1,128]{2,0,1:T(8,128)(2,1)S...) while((s32[]{:T(128)}, ...), condition=%wide.region_4.5_spmd.clone, body=%wide.region_1.4_spmd.clone.sunk | while | flops 548470272 | bytes 13922475 | solution.py:45
  77.3 0.7 dynamic_slice.38
  80.0 0.7 iota_add_fusion.2
  80.8 1.3 fusion.89
  82.0 0.7 fusion.90
  82.8 0.9 fusion.91
  83.7 0.7 dynamic_slice.38
  86.4 0.7 iota_add_fusion.2
  87.1 0.1 dynamic_slice.39
  87.2 1.3 fusion.89
  88.5 0.7 fusion.90
  89.2 0.9 fusion.91
  90.2 0.7 dynamic_slice.38
  92.9 0.7 iota_add_fusion.2
  93.7 1.3 fusion.89
  94.9 0.7 fusion.90
  95.6 0.9 fusion.91
  96.6 0.7 dynamic_slice.38
  99.3 0.7 iota_add_fusion.2
  100.1 1.3 fusion.89
  101.4 0.7 fusion.90
  102.1 0.9 fusion.91
  103.0 6.6 %convolution_convert_fusion = bf16[2048,2048]{1,0:T(8,128)(2,1)} fusion(bf16[2048,128]{1,0:T(8,128)(2,1)S(1)} %bitcast.144, bf16[128,2048]{1,0:T(8,128)(2,1)} %param.25), kind=kOutput, calls=%fused_computation.32 | convolution fusion | flops 1077936128 | bytes 9437184 | tf_op jit(solution)/shard_map/dot_general | solution.py:109
  109.7 0.5 all-gather.5.cloned.1.call-start
  110.2 98.4 %reduce-scatter.3.cloned.1.call-done = bf16[128,2048]{1,0:T(8,128)(2,1)} async-done(((bf16[2048,2048]{1,0:T(8,128)(2,1)}), bf16[128,2048]{1,0:T(8,128)(2,1)}) %reduce-scatter.3.cloned.1.call-update) | async-done | bytes 524304 | tf_op jit(solution)/shard_map/reduce_scatter | solution.py:108
  208.6 1.3 fusion.61
  209.9 2.0 fusion.63
  212.0 0.1 reshape.229
  212.2 0.5 copy.43
  212.7 1.3 copy.41
  214.1 1.7 mul.116
  215.8 23.3 %fusion.78 = s32[16,128,16]{2,0,1:T(8,128)S(1)} fusion(s32[16,128,16]{2,0,1:T(8,128)S(1)} %copy.43), kind=kOutput, calls=%fused_computation.107 | output fusion | flops 4161536 | bytes 262144 | tf_op jit(solution)/shard_map/vmap(jit(cumsum))/reduce_window_sum | solution.py:54
  239.1 1.1 sub.16
  240.2 1.6 copy.45
  241.8 0.2 select_reduce_fusion
  242.1 0.2 copy.46
  242.4 0.1 copy.47
  242.6 0.1 and_reduce_fusion
  242.7 45.4 %scatter_custom_fusion.2 = s32[16384]{0:T(1024)S(1)} fusion(s32[12288]{0:T(1024)S(1)} %reshape.275, s32[12288]{0:T(1024)S(1)} %reshape.277, s32[]{:T(128)} %constant.27.clone.1), kind=kCustom, calls=%fused_computation.84 | custom fusion | bytes 65540
  288.4 6.1 %gather_fusion = bf16[1024,2048]{1,0:T(8,128)(2,1)} fusion(bf16[128,2048]{1,0:T(8,128)(2,1)S(1)} %copy-done.1, s32[1024]{0:T(1024)S(1)} %broadcast_clamp_fusion), kind=kCustom, calls=%fused_computation | custom fusion | bytes 8392704 | tf_op jit(solution)/shard_map/gather | solution.py:145
  294.4 4.7 all-to-all-start
  299.2 0.1 add_reduce_fusion
  299.4 0.4 copy.48
  299.7 0.7 reshape.283
  300.4 45.6 %scatter_custom_fusion.3 = f32[16384]{0:T(1024)S(1)} fusion(s32[12288]{0:T(1024)S(1)} %reshape.275, f32[12288]{0:T(1024)S(1)} %reshape.283, f32[]{:T(128)} %constant.9.clone.1), kind=kCustom, calls=%fused_computation.82 | custom fusion | bytes 65540
  346.2 3.3 all-to-all-done
  349.5 11.7 %fusion.24 = f32[16,64,1408]{2,1,0:T(8,128)} fusion(bf16[1,2048,1408]{2,1,0:T(8,128)(2,1)} %param.31, bf16[16,1,64,2048]{3,2,1,0:T(8,128)(2,1)} %all-to-all-done), kind=kOutput, calls=%fused_computation.37 | convolution fusion | flops 5905580032 | bytes 15728640 | tf_op jit(solution)/shard_map/secd,edf->secf/dot_general | solution.py:69
  361.2 21.0 %fusion.36 = bf16[16,64,2048]{2,1,0:T(8,128)(2,1)} fusion(bf16[1,1408,2048]{2,1,0:T(8,128)(2,1)} %param.32, f32[16,64,1408]{2,1,0:T(8,128)} %fusion.24, bf16[1,2048,1408]{2,1,0:T(8,128)(2,1)} %param.30, bf16[16,1,64,2048]{3,2,1,0:T(8,128)(2,1)} %all-to-all-done), kind=kOutput, calls=%fused_computation.49 | convolution fusion | flops 11821907968 | bytes 25690112 | tf_op jit(solution)/shard_map/secf,efd->secd/dot_general | solution.py:71
  382.2 5.8 %fusion.57 = f32[2048,352]{0,1:T(8,128)S(1)} fusion(bf16[2048,2048]{1,0:T(8,128)(2,1)} %all-gather.5.cloned.1.call-done, bf16[2048,176]{0,1:T(8,128)(2,1)S(1)} %copy-done.11, bf16[2048,176]{0,1:T(8,128)(2,1)} %param.27), kind=kOutput, calls=%fused_computation.62 | convolution fusion | flops 2955673600 | bytes 12713984 | tf_op jit(solution)/shard_map/dot_general | solution.py:136
  388.0 8.1 %fusion.65 = f32[2048,2048]{1,0:T(8,128)} fusion(bf16[176,2048]{1,0:T(8,128)(2,1)S(1)} %copy-done, f32[2048,352]{0,1:T(8,128)S(1)} %fusion.57), kind=kOutput, calls=%fused_computation.75 | convolution fusion | flops 1478557696 | bytes 20381696 | tf_op jit(solution)/shard_map/dot_general | solution.py:152
  396.1 26.5 %scatter_custom_fusion = f32[2048,2048]{1,0:T(8,128)} fusion(f32[2048,2048]{1,0:T(8,128)} %fusion.65, s32[1024]{0:T(1024)S(1)} %bitcast.148, bf16[1024,2048]{1,0:T(8,128)(2,1)} %bitcast.141, f32[1024]{0:T(1024)S(1)} %mul.120), kind=kCustom, calls=%fused_computation.29 | custom fusion | flops 6291456 | bytes 20975616 | tf_op jit(solution)/shard_map/scatter-add | solution.py:155
  422.7 9.1 %convert_element_type.101 = bf16[2048,2048]{1,0:T(8,128)(2,1)} convert(f32[2048,2048]{1,0:T(8,128)} %scatter_custom_fusion) | non-fusion elementwise | flops 4194304 | bytes 25165824 | tf_op jit(solution)/shard_map/convert_element_type | solution.py:157
  431.8 0.6 copy-done.14
  432.4 1.2 maximum_bitcast_fusion
  433.6 1.2 broadcast_in_dim.34
  434.8 3.0 scatter_fusion
  437.8 91.4 %reduce-scatter.5.cloned.1.call-done = bf16[128,2048]{1,0:T(8,128)(2,1)} async-done(((bf16[2048,2048]{1,0:T(8,128)(2,1)}), bf16[128,2048]{1,0:T(8,128)(2,1)}) %reduce-scatter.5.cloned.1.call-update) | async-done | bytes 524304 | tf_op jit(solution)/shard_map/reduce_scatter | solution.py:156
  529.2 2.1 fusion.64
  (65 shorter events, 1.2 us)
Async XLA Ops:
  7.2 380.8 %copy-start = (bf16[176,2048]{1,0:T(8,128)(2,1)S(1)}, bf16[176,2048]{1,0:T(8,128)(2,1)}, u32[]{:S(2)}) copy-start(bf16[176,2048]{1,0:T(8,128)(2,1)} %param.29) | copy-start | bytes 2162692
  7.2 57.1 %all-gather.3.cloned.1.call-start = ((), (), s32[]{:S(2)}) async-start(), calls=%async_computation.3 | async-start | bytes 8912896 | tf_op jit(solution)/shard_map/all_gather | solution.py:101
  7.2 62.3 %copy-start.12 = (bf16[2048,128]{1,0:T(8,128)(2,1)S(1)}, bf16[2048,128]{1,0:T(8,128)(2,1)}, u32[]{:S(2)}) copy-start(bf16[2048,128]{1,0:T(8,128)(2,1)} %param.24) | copy-start | bytes 1572868
  7.9 200.7 %reduce-scatter.3.cloned.1.call-start = ((), (), s32[]{:S(2)}) async-start(), calls=%async_computation.4 | async-start | bytes 8912896 | tf_op jit(solution)/shard_map/reduce_scatter | solution.py:108
  8.0 61.6 %copy-start.13 = (f32[2048]{0:T(1024)S(1)}, f32[2048]{0:T(1024)}, u32[]{:S(2)}) copy-start(f32[2048]{0:T(1024)} %param.21) | copy-start | bytes 24580
  64.3 5.8 %copy-start.2 = (bf16[2048,2048]{1,0:T(8,128)(2,1)S(1)}, bf16[2048,2048]{1,0:T(8,128)(2,1)}, u32[]{:S(2)}) copy-start(bf16[2048,2048]{1,0:T(8,128)(2,1)} %all-gather.3.cloned.1.call-done) | copy-start | bytes 25165828
  76.1 1.2 copy-start.7
  109.6 98.9 %copy-start.3 = (bf16[128,2048]{1,0:T(8,128)(2,1)S(1)}, bf16[128,2048]{1,0:T(8,128)(2,1)}, u32[]{:S(2)}) copy-start(bf16[128,2048]{1,0:T(8,128)(2,1)} %param.19) | copy-start | bytes 1572868
  109.6 100.3 %copy-start.8 = (f32[2048]{0:T(1024)S(1)}, f32[2048]{0:T(1024)}, u32[]{:S(2)}) copy-start(f32[2048]{0:T(1024)} %param.26) | copy-start | bytes 24580
  109.6 102.5 %copy-start.5 = (s32[2048,6]{0,1:T(8,128)S(1)}, s32[2048,6]{0,1:T(8,128)}, u32[]{:S(2)}) copy-start(s32[2048,6]{0,1:T(8,128)} %param.33) | copy-start | bytes 147460
  109.7 272.5 %all-gather.5.cloned.1.call-start = ((), (), s32[]{:S(2)}) async-start(), calls=%async_computation.5 | async-start | bytes 8912896 | tf_op jit(solution)/shard_map/all_gather | solution.py:137
  215.8 26.8 %copy-start.10 = (s32[2]{0:T(128)S(1)}, s32[2]{0:T(128)}, u32[]{:S(2)}) copy-start(s32[2]{0:T(128)} %constant.41) | copy-start | bytes 28
  215.8 26.8 %copy-start.9 = (s32[2]{0:T(128)S(1)}, s32[2]{0:T(128)}, u32[]{:S(2)}) copy-start(s32[2]{0:T(128)} %constant.69) | copy-start | bytes 28
  239.1 49.3 %copy-start.1 = (bf16[128,2048]{1,0:T(8,128)(2,1)S(1)}, bf16[128,2048]{1,0:T(8,128)(2,1)}, u32[]{:S(2)}) copy-start(bf16[128,2048]{1,0:T(8,128)(2,1)} %fusion.63) | copy-start | bytes 1572868
  294.4 4.9 copy-start.6
  294.4 55.0 %all-to-all-start = ((bf16[16,1,64,2048]{3,2,1,0:T(8,128)(2,1)}), bf16[16,1,64,2048]{3,2,1,0:T(8,128)(2,1)}, u32[]{:S(2)}, u32[]{:S(2)}) async-start(bf16[16,1,64,2048]{3,2,1,0:T(8,128)(2,1)} %bitcast.140), calls=%async_computation.1 | async-start | bytes 8388608 | tf_op jit(solution)/shard_map/all_to_all | solution.py:147
  299.1 230.1 %reduce-scatter.5.cloned.1.call-start = ((), (), s32[]{:S(2)}) async-start(), calls=%async_computation.6 | async-start | bytes 8912896 | tf_op jit(solution)/shard_map/reduce_scatter | solution.py:156
  361.2 21.0 %copy-start.11 = (bf16[2048,176]{0,1:T(8,128)(2,1)S(1)}, bf16[2048,176]{0,1:T(8,128)(2,1)}, u32[]{:S(2)}) copy-start(bf16[2048,176]{0,1:T(8,128)(2,1)} %param.28) | copy-start | bytes 2162692
  431.7 0.7 copy-start.14
  432.4 96.8 %copy-start.4 = (bf16[128,2048]{1,0:T(8,128)(2,1)S(1)}, bf16[128,2048]{1,0:T(8,128)(2,1)}, u32[]{:S(2)}) copy-start(bf16[128,2048]{1,0:T(8,128)(2,1)} %reduce-scatter.3.cloned.1.call-done) | copy-start | bytes 1572868
Sparse Core Ops, SparseCore 0:
  9.7 54.5 all-gather.2
  109.8 98.7 reduce-scatter.2
  212.1 50.8 all-gather.4
  431.9 97.2 reduce-scatter.4
where the time goes:
time: 547 us; the launch traced here: 538 us
  waiting for transfers between devices  250 us (46%)
  local copies, waits for them, and re-layouts  114 us (21%)
  other arithmetic  78.1 us (14%)
  matrix products  68 us (12%)
  between operations  14.4 us (3%)
  loops' own time  8.39 us (2%)
    reduce_scatter x1, waiting for transfers between devices, shards(): lax.psum_scatter(jnp.dot(context, output_weight, preferred_element_type=j...  98.4 us
    unnamed x35, local copies, waits for them, and re-layouts  92.6 us
    reduce_scatter x1, waiting for transfers between devices, shards(): lax.psum_scatter(term.astype(jnp.bfloat16), 'tensor', scatter_dimension=0...  91.4 us
    all_gather x1, waiting for transfers between devices, shards(): lax.all_gather(tokens, 'tensor', axis=0, tiled=True)  56.3 us
    scatter-add x1, other arithmetic, shards(): term = term.at[stream_slots].add(weighted)  26.5 us
    another operation x1, other arithmetic, slot_tables(): before = jnp.cumsum(hits, axis=0) - hits  23.3 us
    dot_general x1, matrix products, expert_apply(): jnp.einsum('secf,efd->secd', hidden, expert_down, preferred_element_type=...  21 us
    dot_general x1, matrix products, expert_apply(): jnp.einsum('secd,edf->secf', incoming, expert_up, preferred_element_type=...  11.7 us
  transfers between devices with their start and end apart: 5, of which 4 were waited for; matrix products, arithmetic and copies ran while one was open for 31% of the time, Pallas kernels for 0%

commit v1 on v0

v1 whole, which is shorter than its diff:
```python
import jax
import jax.numpy as jnp
from jax import lax
from jax.sharding import PartitionSpec as P

HD = 128
TOP = 6
PAGE = 128


def rms_scale(hidden, gain):
    widened = hidden.astype(jnp.float32)
    inverse = lax.rsqrt(jnp.mean(widened * widened, axis=-1, keepdims=True) + 1e-06)
    return (widened * inverse * gain).astype(jnp.bfloat16)


def attend(projected, segment_ids, head_count):
    total_tokens = projected.shape[0]
    inner = head_count * HD
    queries = projected[:, :inner].reshape(total_tokens, head_count, HD)
    keys = projected[:, inner : 2 * inner].reshape(total_tokens, head_count, HD)
    values = projected[:, 2 * inner :].reshape(total_tokens, head_count, HD)
    scale = HD ** (-0.5)
    positions = jnp.arange(total_tokens, dtype=jnp.int32)
    span = min(512, total_tokens)

    def one_block(start):
        query_rows = lax.dynamic_slice_in_dim(queries, start, span, 0)
        query_segments = lax.dynamic_slice_in_dim(segment_ids, start, span, 0)
        query_positions = start + jnp.arange(span, dtype=jnp.int32)
        scores = (
            jnp.einsum("qhd,khd->hqk", query_rows, keys, preferred_element_type=jnp.float32) * scale
        )
        allowed = (query_segments[:, None] == segment_ids[None, :]) & (
            positions[None, :] <= query_positions[:, None]
        )
        scores = jnp.where(allowed[None], scores, -jnp.inf)
        highest = jnp.max(scores, axis=-1, keepdims=True)
        weights = jnp.exp(scores - highest)
        probs = (weights / jnp.sum(weights, axis=-1, keepdims=True)).astype(jnp.bfloat16)
        context = jnp.einsum("hqk,khd->qhd", probs, values, preferred_element_type=jnp.float32)
        return context.astype(jnp.bfloat16)

    starts = jnp.arange(total_tokens // span, dtype=jnp.int32) * span
    context = lax.map(one_block, starts).reshape(total_tokens, inner)
    return (context, keys.reshape(total_tokens, inner), values.reshape(total_tokens, inner))


def expert_apply(picked, gate_w, up_w, down_w):
    gate_part = jnp.dot(picked, gate_w, preferred_element_type=jnp.float32)
    upward = jnp.dot(picked, up_w, preferred_element_type=jnp.float32)
    hidden = (jax.nn.silu(gate_part) * upward).astype(jnp.bfloat16)
    return jnp.dot(hidden, down_w, preferred_element_type=jnp.float32).astype(jnp.bfloat16)


def shards(
    tokens,
    segment_ids,
    attention_gain,
    query_weight,
    key_weight,
    value_weight,
    output_weight,
    ffn_gain,
    shared_gate,
    shared_up,
    shared_down,
    expert_gate,
    expert_up,
    expert_down,
    expert_ids,
    gate_weights,
    page_table,
):
    tok_dev = tokens.shape[0]
    groups = lax.axis_size("tensor")
    position = lax.axis_index("tensor")
    inner = query_weight.shape[1]
    head_count = inner // HD
    model_width = tokens.shape[1]

    projection = jnp.concatenate([query_weight, key_weight, value_weight], axis=1)
    normed_all = lax.all_gather(rms_scale(tokens, attention_gain), "tensor", axis=0, tiled=True)
    out_weight_all = lax.all_gather(output_weight, "tensor", axis=0, tiled=True)
    projected = jnp.dot(normed_all, projection, preferred_element_type=jnp.float32).astype(
        jnp.bfloat16
    )
    context, keys, values = attend(projected, segment_ids, head_count)
    cache = jnp.stack([keys, values]).reshape(2, -1, PAGE, inner)
    kv_pages = jnp.zeros_like(cache).at[:, page_table].set(cache)

    received = lax.all_to_all(
        context.reshape(groups, tok_dev, inner), "tensor", split_axis=0, concat_axis=0, tiled=True
    )
    partials = jnp.einsum(
        "gtd,gdo->gto",
        received,
        out_weight_all.reshape(groups, inner, model_width),
        preferred_element_type=jnp.float32,
    ).astype(jnp.bfloat16)
    attention = jnp.sum(partials.astype(jnp.float32), axis=0)
    residual = (tokens.astype(jnp.float32) + attention).astype(jnp.bfloat16)
    normed_ffn = rms_scale(residual, ffn_gain)
    normed_stream = lax.all_gather(normed_ffn, "tensor", axis=0, tiled=True)

    shared_columns = jnp.concatenate([shared_gate, shared_up], axis=1)
    shared_width = shared_gate.shape[1]
    joined = jnp.dot(normed_stream, shared_columns, preferred_element_type=jnp.float32)
    hidden_all = (jax.nn.silu(joined[:, :shared_width]) * joined[:, shared_width:]).astype(
        jnp.bfloat16
    )
    term = jnp.dot(hidden_all, shared_down, preferred_element_type=jnp.float32)

    local_experts = expert_gate.shape[0]
    expert_count = local_experts * groups
    capacity = tok_dev * TOP // expert_count + tok_dev // 8
    id_blocks = expert_ids.reshape(groups, tok_dev, -1)
    gate_blocks = gate_weights.reshape(groups, tok_dev, -1)
    token_blocks = normed_stream.reshape(groups, tok_dev, model_width)
    slots = jnp.arange(capacity, dtype=jnp.int32)
    for local in range(local_experts):
        expert = position * local_experts + local
        chosen = id_blocks == expert
        hits = jnp.sum(chosen.astype(jnp.int32), axis=2)
        weight = jnp.sum(jnp.where(chosen, gate_blocks, 0.0), axis=2)
        rank = jnp.cumsum(hits, axis=1) - hits
        onehot = ((hits[:, None, :] > 0) & (rank[:, None, :] == slots[None, :, None])).astype(
            jnp.bfloat16
        )
        picked = jnp.einsum(
            "bst,btd->bsd", onehot, token_blocks, preferred_element_type=jnp.float32
        ).astype(jnp.bfloat16)
        rows = expert_apply(
            picked.reshape(-1, model_width),
            expert_gate[local],
            expert_up[local],
            expert_down[local],
        )
        back = jnp.einsum(
            "bst,bsd->btd",
            onehot,
            rows.reshape(groups, capacity, model_width),
            preferred_element_type=jnp.float32,
        )
        term = term + weight.reshape(-1, 1) * back.reshape(-1, model_width)
    ffn_out = lax.psum_scatter(
        term.astype(jnp.bfloat16), "tensor", scatter_dimension=0, tiled=True
    ).astype(jnp.float32)
    layer_out = (residual.astype(jnp.float32) + ffn_out).astype(jnp.bfloat16)
    return (layer_out, kv_pages)


def solution(mesh):
    placed = (
        P(("dp", "tensor"), None),
        P("dp"),
        P(),
        P(None, "tensor"),
        P(None, "tensor"),
        P(None, "tensor"),
        P("tensor", None),
        P(),
        P(None, "tensor"),
        P(None, "tensor"),
        P("tensor", None),
        P("tensor", None, None),
        P("tensor", None, None),
        P("tensor", None, None),
        P("dp", None),
        P("dp", None),
        P("dp"),
    )
    return jax.shard_map(
        shards,
        mesh=mesh,
        in_specs=placed,
        out_specs=(P(("dp", "tensor"), None), P(None, "dp", None, "tensor")),
        check_vma=False,
    )
```

time: 547 us -> 357 us (0.65); the launches traced: 538 us -> 356 us
  local copies, waits for them, and re-layouts: 114 us -> 7.84 us
  other arithmetic: 78.1 us -> 12.4 us
  waiting for transfers between devices: 250 us -> 223 us
  matrix products: 68 us -> 85.8 us
    reduce_scatter x1 -> x0, waiting for transfers between devices: 98.4 us -> none  [shards(): lax.psum_scatter(jnp.dot(context, output_weight, preferred_element_type=j...]
    unnamed x35 -> x22, local copies, waits for them, and re-layouts: 92.6 us -> 3.01 us
    all_gather x2 -> x3, waiting for transfers between devices: 56.3 us -> 126 us  [the longest x1 53.9 us: shards(): lax.all_gather(rms_scale(tokens, attention_gain), 'tensor', axis=0, tiled...]
    scatter-add x1 -> x0, other arithmetic: 26.5 us -> none  [shards(): term = term.at[stream_slots].add(weighted)]
    another operation x1, other arithmetic: 23.3 us -> 0.28 us  [shards(): rank = jnp.cumsum(hits, axis=1) - hits]
    dot_general x5 -> x7, matrix products: 51.1 us -> 65.5 us  [the longest x1 20.5 us: expert_apply(): jnp.dot(hidden, down_w, preferred_element_type=jnp.float32)]
    convert_element_type x1 -> x0, other arithmetic: 9.08 us -> none  [shards(): term.astype(jnp.bfloat16)]
    gather x1 -> x0, local copies, waits for them, and re-layouts: 6.07 us -> none  [shards(): normed_ffn[own_slots.reshape(-1)]]
  transfers between devices with their start and end apart: 5 -> 5, of which waited for: 4 -> 4; matrix products, arithmetic and copies ran while one was open for 31% -> 8% of each run, Pallas kernels for 0% -> 0%
where the time goes in v1:
time: 357 us; the launch traced here: 356 us
  waiting for transfers between devices  223 us (62%)
  matrix products  85.8 us (24%)
  between operations  13.9 us (4%)
  other arithmetic  12.4 us (3%)
  local copies, waits for them, and re-layouts  7.84 us (2%)
  loops' own time  7.82 us (2%)
  starting transfers between devices  5.11 us (1%)
    reduce_scatter x1, waiting for transfers between devices, shards(): lax.psum_scatter(term.astype(jnp.bfloat16), 'tensor', scatter_dimension=0...  96.3 us
    all_gather x1, waiting for transfers between devices, shards(): lax.all_gather(rms_scale(tokens, attention_gain), 'tensor', axis=0, tiled...  53.9 us
    all_gather x1, waiting for transfers between devices, shards(): normed_stream = lax.all_gather(normed_ffn, 'tensor', axis=0, tiled=True)  52.8 us
    dot_general x1, matrix products, expert_apply(): jnp.dot(hidden, down_w, preferred_element_type=jnp.float32)  20.5 us
    all_gather x1, waiting for transfers between devices, shards(): out_weight_all = lax.all_gather(output_weight, 'tensor', axis=0, tiled=True)  19.4 us
    dot_general x1, matrix products, shards(): jnp.einsum('bst,bsd->btd', onehot, rows.reshape(groups, capacity, model_w...  10.4 us
    dot_general x1, matrix products, expert_apply(): gate_part = jnp.dot(picked, gate_w, preferred_element_type=jnp.float32)  10.3 us
    dot_general x1, matrix products, shards(): term = jnp.dot(hidden_all, shared_down, preferred_element_type=jnp.float32)  9.15 us
  transfers between devices with their start and end apart: 5, of which 4 were waited for; matrix products, arithmetic and copies ran while one was open for 8% of the time, Pallas kernels for 0%

profile of v1, /device:TPU:0, one launch (start us, length us, event | category | flops | bytes accessed | tf_op | source)
XLA Modules:
  0.0 356.1 jit_solution(2284777152955340523)
XLA Ops:
  7.2 0.0 copy-start
  7.2 0.0 all-gather.4.cloned.1.call-start
  7.2 1.3 fusion.41
  8.5 2.0 fusion.43
  10.6 0.0 all-gather.4.cloned.1.call-update
  10.6 0.0 all-gather.6.cloned.1.call-start
  10.6 0.7 all-gather.6.cloned.1.call-update
  11.3 53.9 %all-gather.4.cloned.1.call-done = bf16[2048,2048]{1,0:T(8,128)(2,1)} async-done(((bf16[128,2048]{1,0:T(8,128)(2,1)}), bf16[2048,2048]{1,0:T(8,128)(2,1)}) %all-gather.4.cloned.1.call-update) | async-done | bytes 8388624 | tf_op jit(solution)/shard_map/all_gather | solution.py:83
  65.3 8.3 %convolution_convert_fusion.1 = bf16[2048,384]{1,0:T(8,128)(2,1)S(1)} fusion(bf16[2048,2048]{1,0:T(8,128)(2,1)} %all-gather.4.cloned.1.call-done, bf16[2048,128]{1,0:T(8,128)(2,1)} %param.24, bf16[2048,128]{1,0:T(8,128)(2,1)} %param.23, bf16[2048,128]{1,0:T(8,128)(2,1)} %param.22), kind=kOutput, calls=%fused_computation.32 | convolution fusion | flops 3226730496 | bytes 11534336 | tf_op jit(solution)/shard_map/dot_general | solution.py:85
  73.6 0.0 copy-start.6
  73.6 0.4 fusion.65
  73.9 0.3 copy-done.6
  74.3 27.1 %while.11 = (s32[]{:T(128)}, bf16[4,512,1,128]{3,1,2,0:T(8,128)(2,1)}, s32[4]{0:T(128)S(1)}, s32[2048]{0:T(1024)S(1)}, bf16[2048,1,128]{2,0,1:T(8,128)(2,1)S(1)}...) while((s32[]{:T(128)}, ...), condition=%wide.region_4.5_spmd.clone, body=%wide.region_1.4_spmd.clone.sunk | while | flops 548470272 | bytes 13922475 | solution.py:45
  74.3 0.6 dynamic_slice.23
  76.8 0.7 iota_add_fusion.2
  77.4 0.1 dynamic_slice.24
  77.5 1.3 fusion.80
  78.8 0.7 fusion.81
  79.5 1.5 fusion.82
  81.0 0.6 dynamic_slice.23
  83.6 0.6 iota_add_fusion.2
  84.2 0.1 dynamic_slice.24
  84.3 1.3 fusion.80
  85.5 0.7 fusion.81
  86.3 1.5 fusion.82
  87.8 0.6 dynamic_slice.23
  90.3 0.6 iota_add_fusion.2
  91.0 0.1 dynamic_slice.24
  91.1 1.3 fusion.80
  92.3 0.7 fusion.81
  93.0 1.5 fusion.82
  94.6 0.6 dynamic_slice.23
  97.1 0.6 iota_add_fusion.2
  97.8 0.1 dynamic_slice.24
  97.8 1.3 fusion.80
  99.1 0.7 fusion.81
  99.8 1.5 fusion.82
  101.3 4.9 %all-to-all-start = ((bf16[16,128,128]{2,1,0:T(8,128)(2,1)}), bf16[16,128,128]{2,1,0:T(8,128)(2,1)S(1)}, u32[]{:S(2)}, u32[]{:S(2)}) async-start(bf16[16,128,128]{2,1,0:T(8,128)(2,1)} %bitcast.3), calls=%async_computation | async-start | bytes 1048576 | tf_op jit(solution)/shard_map/all_to_all | solution.py:92
  106.3 0.0 all-gather.8.cloned.1.call-start
  106.3 19.4 %all-gather.6.cloned.1.call-done = bf16[2048,2048]{1,0:T(8,128)(2,1)} async-done(((bf16[128,2048]{1,0:T(8,128)(2,1)}), bf16[2048,2048]{1,0:T(8,128)(2,1)}) %all-gather.6.cloned.1.call-update) | async-done | bytes 8388624 | tf_op jit(solution)/shard_map/all_gather | solution.py:84
  125.7 0.0 all-to-all-done
  125.7 0.0 copy-start.5
  125.7 5.8 %convert_reduce_fusion = f32[128,2048]{1,0:T(8,128)S(1)} fusion(bf16[16,128,128]{2,1,0:T(8,128)(2,1)S(1)} %all-to-all-done, bf16[16,128,2048]{2,1,0:T(8,128)(2,1)} %bitcast.90), kind=kOutput, calls=%fused_computation.21 | convolution fusion | flops 1086062592 | bytes 9961472 | tf_op jit(solution)/shard_map/gtd,gdo->gto/dot_general | solution.py:95
  131.6 0.2 fusion.45
  131.8 1.0 fusion.47
  132.8 0.0 all-gather.8.cloned.1.call-update
  132.8 0.0 reduce-scatter.2.cloned.1.call-start
  133.0 0.3 reduce_window_sum.11
  133.3 52.8 %all-gather.8.cloned.1.call-done = bf16[2048,2048]{1,0:T(8,128)(2,1)} async-done(((bf16[128,2048]{1,0:T(8,128)(2,1)}), bf16[2048,2048]{1,0:T(8,128)(2,1)}) %all-gather.8.cloned.1.call-update) | async-done | bytes 8388624 | tf_op jit(solution)/shard_map/all_gather | solution.py:104
  186.0 4.6 %convolution_convert_fusion = bf16[16,64,2048]{2,1,0:T(8,128)(2,1)S(1)} fusion(bf16[16,128,2048]{2,1,0:T(8,128)(2,1)} %bitcast.89, s32[16,128]{1,0:T(8,128)S(1)} %bitcast_subtract_fusion, pred[16,128]{1,0:T(8,128)(4,1)S(1)} %broadcast_compare_fusion.1), kind=kOutput, calls=%fused_computation.29 | convolution fusion | flops 539230208 | bytes 12593152 | tf_op jit(solution)/shard_map/bst,btd->bsd/dot_general | solution.py:130
  190.7 2.0 copy-done.1
  192.7 10.3 %fusion.19 = f32[1024,1408]{1,0:T(8,128)} fusion(bf16[1024,2048]{1,0:T(8,128)(2,1)S(1)} %bitcast.92, bf16[1,2048,1408]{2,1,0:T(8,128)(2,1)} %param.30), kind=kOutput, calls=%fused_computation.26 | convolution fusion | flops 5905580032 | bytes 15728640 | tf_op jit(solution)/shard_map/dot_general | solution.py:50
  203.0 20.5 %fusion.25 = bf16[1024,2048]{1,0:T(8,128)(2,1)} fusion(bf16[1,1408,2048]{2,1,0:T(8,128)(2,1)} %param.32, f32[1024,1408]{1,0:T(8,128)} %fusion.19, bf16[1024,2048]{1,0:T(8,128)(2,1)} %bitcast.93, bf16[1,2048,1408]{2,1,0:T(8,128)(2,1)} %param.31), kind=kOutput, calls=%fused_computation.30 | convolution fusion | flops 11821907968 | bytes 25690112 | tf_op jit(solution)/shard_map/dot_general | solution.py:53
  223.5 10.4 %fusion.52 = f32[16,128,2048]{2,1,0:T(8,128)} fusion(bf16[16,64,2048]{2,1,0:T(8,128)(2,1)} %bitcast.91, s32[16,128]{1,0:T(8,128)S(1)} %bitcast_subtract_fusion, pred[16,128]{1,0:T(8,128)(4,1)S(1)} %broadcast_compare_fusion.1), kind=kOutput, calls=%fused_computation.63 | convolution fusion | flops 537133056 | bytes 20981760 | tf_op jit(solution)/shard_map/bst,bsd->btd/dot_general | solution.py:139
  233.9 5.6 %fusion.37 = f32[2048,352]{0,1:T(8,128)S(1)} fusion(bf16[2048,2048]{1,0:T(8,128)(2,1)} %all-gather.8.cloned.1.call-done, bf16[2048,176]{0,1:T(8,128)(2,1)S(1)} %copy-done.8, bf16[2048,176]{0,1:T(8,128)(2,1)S(1)} %copy-done.9), kind=kOutput, calls=%fused_computation.46 | convolution fusion | flops 2955673600 | bytes 12713984 | tf_op jit(solution)/shard_map/dot_general | solution.py:108
  239.5 9.1 %fusion.14 = bf16[2048,2048]{1,0:T(8,128)(2,1)} fusion(f32[16,128,2048]{2,1,0:T(8,128)} %fusion.52, bf16[176,2048]{1,0:T(8,128)(2,1)S(1)} %copy-done, f32[2048]{0:T(1024)S(1)} %get-tuple-element.82, f32[2048,352]{0,1:T(8,128)S(1)} %fusion.37), kind=kOutput, calls=%fused_computation.20 | convolution fusion | flops 1491140608 | bytes 28778496 | tf_op jit(solution)/shard_map/dot_general | solution.py:112
  248.7 0.0 reduce-scatter.2.cloned.1.call-update
  248.7 0.6 copy-done.10
  249.4 0.1 maximum_bitcast_fusion
  249.5 0.2 broadcast_in_dim.27
  249.7 1.6 scatter_fusion
  251.3 0.0 copy-start.3
  251.3 96.3 %reduce-scatter.2.cloned.1.call-done = bf16[128,2048]{1,0:T(8,128)(2,1)} async-done(((bf16[2048,2048]{1,0:T(8,128)(2,1)}), bf16[128,2048]{1,0:T(8,128)(2,1)}) %reduce-scatter.2.cloned.1.call-update) | async-done | bytes 524304 | tf_op jit(solution)/shard_map/reduce_scatter | solution.py:146
  347.6 2.0 fusion.48
  (24 shorter events, 0.1 us)
Async XLA Ops:
  7.2 232.4 %copy-start = (bf16[176,2048]{1,0:T(8,128)(2,1)S(1)}, bf16[176,2048]{1,0:T(8,128)(2,1)}, u32[]{:S(2)}) copy-start(bf16[176,2048]{1,0:T(8,128)(2,1)} %param.29) | copy-start | bytes 2162692
  7.2 58.1 %all-gather.4.cloned.1.call-start = ((), (), s32[]{:S(2)}) async-start(), calls=%async_computation.2 | async-start | bytes 8912896 | tf_op jit(solution)/shard_map/all_gather | solution.py:83
  10.6 115.1 %all-gather.6.cloned.1.call-start = ((), (), s32[]{:S(2)}) async-start(), calls=%async_computation.3 | async-start | bytes 8912896 | tf_op jit(solution)/shard_map/all_gather | solution.py:84
  73.6 0.7 copy-start.6
  101.3 24.4 %all-to-all-start = ((bf16[16,128,128]{2,1,0:T(8,128)(2,1)}), bf16[16,128,128]{2,1,0:T(8,128)(2,1)S(1)}, u32[]{:S(2)}, u32[]{:S(2)}) async-start(bf16[16,128,128]{2,1,0:T(8,128)(2,1)} %bitcast.3), calls=%async_computation | async-start | bytes 1048576 | tf_op jit(solution)/shard_map/all_to_all | solution.py:92
  106.3 79.7 %all-gather.8.cloned.1.call-start = ((), (), s32[]{:S(2)}) async-start(), calls=%async_computation.4 | async-start | bytes 8912896 | tf_op jit(solution)/shard_map/all_gather | solution.py:104
  125.7 5.8 %copy-start.2 = (bf16[128,2048]{1,0:T(8,128)(2,1)S(1)}, bf16[128,2048]{1,0:T(8,128)(2,1)}, u32[]{:S(2)}) copy-start(bf16[128,2048]{1,0:T(8,128)(2,1)} %param.19) | copy-start | bytes 1572868
  125.7 6.1 %copy-start.7 = (f32[2048]{0:T(1024)S(1)}, f32[2048]{0:T(1024)}, u32[]{:S(2)}) copy-start(f32[2048]{0:T(1024)} %param.26) | copy-start | bytes 24580
  125.7 7.2 %copy-start.4 = (f32[2048,6]{0,1:T(8,128)S(1)}, f32[2048,6]{0,1:T(8,128)}, u32[]{:S(2)}) copy-start(f32[2048,6]{0,1:T(8,128)} %param.34) | copy-start | bytes 147460
  125.7 7.2 %copy-start.5 = (s32[2048,6]{0,1:T(8,128)S(1)}, s32[2048,6]{0,1:T(8,128)}, u32[]{:S(2)}) copy-start(s32[2048,6]{0,1:T(8,128)} %param.33) | copy-start | bytes 147460
  132.8 214.8 %reduce-scatter.2.cloned.1.call-start = ((), (), s32[]{:S(2)}) async-start(), calls=%async_computation.5 | async-start | bytes 8912896 | tf_op jit(solution)/shard_map/reduce_scatter | solution.py:146
  190.7 2.0 copy-start.1
  223.5 10.4 %copy-start.8 = (bf16[2048,176]{0,1:T(8,128)(2,1)S(1)}, bf16[2048,176]{0,1:T(8,128)(2,1)}, u32[]{:S(2)}) copy-start(bf16[2048,176]{0,1:T(8,128)(2,1)} %param.28) | copy-start | bytes 2162692
  223.5 10.4 %copy-start.9 = (bf16[2048,176]{0,1:T(8,128)(2,1)S(1)}, bf16[2048,176]{0,1:T(8,128)(2,1)}, u32[]{:S(2)}) copy-start(bf16[2048,176]{0,1:T(8,128)(2,1)} %param.27) | copy-start | bytes 2162692
  248.7 0.7 copy-start.10
  251.3 98.3 %copy-start.3 = (bf16[2,16,128,128]{3,2,1,0:T(8,128)(2,1)}, bf16[2,16,128,128]{3,2,1,0:T(8,128)(2,1)S(1)}, u32[]{:S(2)}) copy-start(bf16[2,16,128,128]{3,2,1,0:T(8,128)(2,1)S(1)} %scatter_fusion) | copy-start | bytes 3145732
Sparse Core Ops, SparseCore 0:
  10.7 54.5 all-gather.3
  67.0 58.6 all-gather.5
  132.9 53.0 all-gather.7
  248.8 98.7 reduce-scatter.1

commit v2 on v1

--- a/solution.py
+++ b/solution.py
@@ -51,6 +51,50 @@
     upward = jnp.dot(picked, up_w, preferred_element_type=jnp.float32)
     hidden = (jax.nn.silu(gate_part) * upward).astype(jnp.bfloat16)
     return jnp.dot(hidden, down_w, preferred_element_type=jnp.float32).astype(jnp.bfloat16)
+
+
+def ring_reduce_scatter(partial, groups):
+    ring = groups // 4
+    rows = partial.shape[0] // groups
+    width = partial.shape[1]
+    me = lax.axis_index("tensor")
+    y = me // 4
+    side = (me // 2) % 2
+    core = me % 2
+    blocks = partial.reshape(ring, 2, 2, rows, width)
+    core_pairs = [(t, t ^ 1) for t in range(groups)]
+    keep = lax.dynamic_index_in_dim(blocks, core, axis=2, keepdims=False)
+    give = lax.dynamic_index_in_dim(blocks, 1 - core, axis=2, keepdims=False)
+    got = lax.ppermute(give, "tensor", core_pairs)
+    summed = keep.astype(jnp.float32) + got.astype(jnp.float32)
+    half = width // 2
+    forward_part = summed[..., :half]
+    backward_part = summed[..., half:]
+    forward_pairs = [(t, ((t // 4 + 1) % ring) * 4 + t % 4) for t in range(groups)]
+    backward_pairs = [(t, ((t // 4 + ring - 1) % ring) * 4 + t % 4) for t in range(groups)]
+    carry_f = lax.dynamic_index_in_dim(forward_part, (y + ring - 1) % ring, 0, False)
+    carry_b = lax.dynamic_index_in_dim(backward_part, (y + 1) % ring, 0, False)
+    carry_f = carry_f.astype(jnp.bfloat16)
+    carry_b = carry_b.astype(jnp.bfloat16)
+    for step in range(ring - 1):
+        recv_f = lax.ppermute(carry_f, "tensor", forward_pairs)
+        recv_b = lax.ppermute(carry_b, "tensor", backward_pairs)
+        index_f = (y + 2 * ring - step - 2) % ring
+        index_b = (y + step + 2) % ring
+        acc_f = recv_f.astype(jnp.float32) + lax.dynamic_index_in_dim(
+            forward_part, index_f, 0, False
+        )
+        acc_b = recv_b.astype(jnp.float32) + lax.dynamic_index_in_dim(
+            backward_part, index_b, 0, False
+        )
+        carry_f = acc_f.astype(jnp.bfloat16)
+        carry_b = acc_b.astype(jnp.bfloat16)
+    mine = jnp.concatenate([acc_f, acc_b], axis=-1)
+    side_pairs = [(t, t ^ 2) for t in range(groups)]
+    keep_side = lax.dynamic_index_in_dim(mine, side, 0, False)
+    give_side = lax.dynamic_index_in_dim(mine, 1 - side, 0, False).astype(jnp.bfloat16)
+    got_side = lax.ppermute(give_side, "tensor", side_pairs)
+    return keep_side + got_side.astype(jnp.float32)
 
 
 def shards(
@@ -141,11 +185,9 @@
             onehot,
             rows.reshape(groups, capacity, model_width),
             preferred_element_type=jnp.float32,
-        )
-        term = term + weight.reshape(-1, 1) * back.reshape(-1, model_width)
-    ffn_out = lax.psum_scatter(
-        term.astype(jnp.bfloat16), "tensor", scatter_dimension=0, tiled=True
-    ).astype(jnp.float32)
+        ).astype(jnp.bfloat16)
+        term = term + weight.reshape(-1, 1) * back.reshape(-1, model_width).astype(jnp.float32)
+    ffn_out = ring_reduce_scatter(term.astype(jnp.bfloat16), groups)
     layer_out = (residual.astype(jnp.float32) + ffn_out).astype(jnp.bfloat16)
     return (layer_out, kv_pages)
 

time: 357 us -> 335 us (0.938)
  waiting for transfers between devices: 223 us -> 168 us
  other arithmetic: 12.4 us -> 28.9 us
  local copies, waits for them, and re-layouts: 7.84 us -> 22.3 us
  starting transfers between devices: 5.11 us -> 16.8 us
  matrix products: 85.8 us -> 77.1 us
    reduce_scatter x1 -> x0, waiting for transfers between devices: 96.3 us -> none  [shards(): lax.psum_scatter(term.astype(jnp.bfloat16), 'tensor', scatter_dimension=0...]
    ppermute x0 -> x8, waiting for transfers between devices: none -> 40.1 us  [the longest x3 29.3 us: ring_reduce_scatter(): recv_f = lax.ppermute(carry_f, 'tensor', forward_pairs)]
    ppermute x0 -> x8, starting transfers between devices: none -> 11.7 us  [the longest x3 8.13 us: ring_reduce_scatter(): recv_b = lax.ppermute(carry_b, 'tensor', backward_pairs)]
    add x0 -> x3, other arithmetic: none -> 8.22 us  [the longest x1 5.37 us: ring_reduce_scatter(): summed = keep.astype(jnp.float32) + got.astype(jnp.float32)]
    convert_element_type x0 -> x5, other arithmetic: none -> 6.36 us  [the longest x2 2.74 us: ring_reduce_scatter(): carry_b = acc_b.astype(jnp.bfloat16)]
    dot_general x1, matrix products: 10.4 us -> 4.67 us  [shards(): jnp.einsum('bst,bsd->btd', onehot, rows.reshape(groups, capacity, model_w...]
    dot_general x1, matrix products: 9.15 us -> 5.08 us  [shards(): term = jnp.dot(hidden_all, shared_down, preferred_element_type=jnp.float32)]
    unnamed x22 -> x32, local copies, waits for them, and re-layouts: 3.01 us -> 6.77 us
  transfers between devices with their start and end apart: 5 -> 12, of which waited for: 4 -> 8; matrix products, arithmetic and copies ran while one was open for 8% -> 13% of each run, Pallas kernels for 0% -> 0%
where the time goes in v2:
time: 335 us; the launch traced here: 334 us
  waiting for transfers between devices  168 us (50%)
  matrix products  77.1 us (23%)
  other arithmetic  28.9 us (9%)
  local copies, waits for them, and re-layouts  22.3 us (7%)
  starting transfers between devices  16.8 us (5%)
  between operations  14.1 us (4%)
  loops' own time  6.62 us (2%)
    all_gather x1, waiting for transfers between devices, shards(): lax.all_gather(rms_scale(tokens, attention_gain), 'tensor', axis=0, tiled...  53.9 us
    all_gather x1, waiting for transfers between devices, shards(): normed_stream = lax.all_gather(normed_ffn, 'tensor', axis=0, tiled=True)  52.8 us
    ppermute x3, waiting for transfers between devices, ring_reduce_scatter(): recv_f = lax.ppermute(carry_f, 'tensor', forward_pairs)  29.3 us
    dot_general x1, matrix products, expert_apply(): jnp.dot(hidden, down_w, preferred_element_type=jnp.float32)  20.6 us
    all_gather x1, waiting for transfers between devices, shards(): out_weight_all = lax.all_gather(output_weight, 'tensor', axis=0, tiled=True)  20.4 us
    dot_general x1, matrix products, expert_apply(): gate_part = jnp.dot(picked, gate_w, preferred_element_type=jnp.float32)  8.53 us
    dot_general x1, matrix products, shards(): jnp.dot(normed_all, projection, preferred_element_type=jnp.float32)  8.26 us
    dot_general x1, matrix products, shards(): jnp.dot(normed_stream, shared_columns, preferred_element_type=jnp.float32)  8.22 us
  transfers between devices with their start and end apart: 12, of which 8 were waited for; matrix products, arithmetic and copies ran while one was open for 13% of the time, Pallas kernels for 0%

profile of v2, /device:TPU:0, one launch (start us, length us, event | category | flops | bytes accessed | tf_op | source)
XLA Modules:
  0.0 333.8 jit_solution(16244621082198498756)
XLA Ops:
  7.2 1.3 fusion.41
  8.5 2.0 fusion.43
  10.6 0.7 all-gather.6.cloned.1.call-update
  11.3 53.9 %all-gather.4.cloned.1.call-done = bf16[2048,2048]{1,0:T(8,128)(2,1)} async-done(((bf16[128,2048]{1,0:T(8,128)(2,1)}), bf16[2048,2048]{1,0:T(8,128)(2,1)}) %all-gather.4.cloned.1.call-update) | async-done | bytes 8388624 | tf_op jit(solution)/shard_map/all_gather | solution.py:127
  65.3 8.3 %convolution_convert_fusion.2 = bf16[2048,384]{1,0:T(8,128)(2,1)S(1)} fusion(bf16[2048,2048]{1,0:T(8,128)(2,1)} %all-gather.4.cloned.1.call-done, bf16[2048,128]{1,0:T(8,128)(2,1)} %param.24, bf16[2048,128]{1,0:T(8,128)(2,1)} %param.23, bf16[2048,128]{1,0:T(8,128)(2,1)} %param.22), kind=kOutput, calls=%fused_computation.35 | convolution fusion | flops 3226730496 | bytes 11534336 | tf_op jit(solution)/shard_map/dot_general | solution.py:129
  73.6 1.3 fusion.77
  74.9 25.4 %while.11 = (s32[]{:T(128)}, bf16[4,512,1,128]{3,1,2,0:T(8,128)(2,1)}, s32[4]{0:T(128)S(1)}, s32[2048]{0:T(1024)S(1)}, bf16[2048,1,128]{2,0,1:T(8,128)(2,1)S(1)}...) while((s32[]{:T(128)}, ...), condition=%wide.region_4.5_spmd.clone, body=%wide.region_1.4_spmd.clone.sunk | while | flops 548470272 | bytes 13922475 | solution.py:45
  74.9 0.6 dynamic_slice.116
  77.8 1.3 fusion.92
  79.0 0.7 fusion.93
  79.7 1.5 fusion.94
  81.3 0.6 dynamic_slice.116
  84.1 1.3 fusion.92
  85.4 0.7 fusion.93
  86.1 1.5 fusion.94
  87.6 0.6 dynamic_slice.116
  90.4 1.3 fusion.92
  91.7 0.7 fusion.93
  92.4 1.5 fusion.94
  93.9 0.6 dynamic_slice.116
  96.1 0.5 iota_add_fusion.2
  96.8 1.3 fusion.92
  98.0 0.7 fusion.93
  98.7 1.5 fusion.94
  100.3 4.9 %all-to-all-start = ((bf16[16,128,128]{2,1,0:T(8,128)(2,1)}), bf16[16,128,128]{2,1,0:T(8,128)(2,1)S(1)}, u32[]{:S(2)}, u32[]{:S(2)}) async-start(bf16[16,128,128]{2,1,0:T(8,128)(2,1)} %bitcast.3), calls=%async_computation | async-start | bytes 1048576 | tf_op jit(solution)/shard_map/all_to_all | solution.py:136
  105.3 20.4 %all-gather.6.cloned.1.call-done = bf16[2048,2048]{1,0:T(8,128)(2,1)} async-done(((bf16[128,2048]{1,0:T(8,128)(2,1)}), bf16[2048,2048]{1,0:T(8,128)(2,1)}) %all-gather.6.cloned.1.call-update) | async-done | bytes 8388624 | tf_op jit(solution)/shard_map/all_gather | solution.py:128
  125.7 5.8 %convert_reduce_fusion = f32[128,2048]{1,0:T(8,128)S(1)} fusion(bf16[16,128,128]{2,1,0:T(8,128)(2,1)S(1)} %all-to-all-done, bf16[16,128,2048]{2,1,0:T(8,128)(2,1)} %bitcast.126), kind=kOutput, calls=%fused_computation.21 | convolution fusion | flops 1086062592 | bytes 9961472 | tf_op jit(solution)/shard_map/gtd,gdo->gto/dot_general | solution.py:139
  131.8 0.8 copy-done.5
  132.6 1.0 fusion.47
  134.1 52.8 %all-gather.8.cloned.1.call-done = bf16[2048,2048]{1,0:T(8,128)(2,1)} async-done(((bf16[128,2048]{1,0:T(8,128)(2,1)}), bf16[2048,2048]{1,0:T(8,128)(2,1)}) %all-gather.8.cloned.1.call-update) | async-done | bytes 8388624 | tf_op jit(solution)/shard_map/all_gather | solution.py:148
  186.9 4.8 %convolution_convert_fusion.1 = bf16[16,64,2048]{2,1,0:T(8,128)(2,1)S(1)} fusion(bf16[16,128,2048]{2,1,0:T(8,128)(2,1)} %bitcast.125, s32[16,128]{1,0:T(8,128)S(1)} %bitcast_subtract_fusion, pred[16,128]{1,0:T(8,128)(4,1)S(1)} %broadcast_compare_fusion.1), kind=kOutput, calls=%fused_computation.32 | convolution fusion | flops 539230208 | bytes 12593152 | tf_op jit(solution)/shard_map/bst,btd->bsd/dot_general | solution.py:174
  191.7 2.0 copy-done.2
  193.7 8.5 %fusion.19 = f32[1024,1408]{1,0:T(8,128)} fusion(bf16[1024,2048]{1,0:T(8,128)(2,1)S(1)} %bitcast.127, bf16[1,2048,1408]{2,1,0:T(8,128)(2,1)S(1)} %bitcast.137), kind=kOutput, calls=%fused_computation.27 | convolution fusion | flops 5905580032 | bytes 15728640 | tf_op jit(solution)/shard_map/dot_general | solution.py:50
  202.2 20.6 %fusion.25 = bf16[1024,2048]{1,0:T(8,128)(2,1)} fusion(bf16[1,1408,2048]{2,1,0:T(8,128)(2,1)} %param.32, f32[1024,1408]{1,0:T(8,128)} %fusion.19, bf16[1024,2048]{1,0:T(8,128)(2,1)} %bitcast.128, bf16[1,2048,1408]{2,1,0:T(8,128)(2,1)} %param.31), kind=kOutput, calls=%fused_computation.33 | convolution fusion | flops 11821907968 | bytes 25690112 | tf_op jit(solution)/shard_map/dot_general | solution.py:53
  222.8 4.7 %convolution_convert_fusion = bf16[16,128,2048]{2,1,0:T(8,128)(2,1)S(1)} fusion(bf16[16,64,2048]{2,1,0:T(8,128)(2,1)} %bitcast.132, s32[16,128]{1,0:T(8,128)S(1)} %bitcast_subtract_fusion, pred[16,128]{1,0:T(8,128)(4,1)S(1)} %broadcast_compare_fusion.1), kind=kOutput, calls=%fused_computation.30 | convolution fusion | flops 541327360 | bytes 12593152 | tf_op jit(solution)/shard_map/bst,bsd->btd/dot_general | solution.py:183
  227.5 8.2 %fusion.37 = f32[2048,352]{0,1:T(8,128)} fusion(bf16[2048,2048]{1,0:T(8,128)(2,1)} %all-gather.8.cloned.1.call-done, bf16[2048,176]{0,1:T(8,128)(2,1)S(1)} %copy-done.11, bf16[2048,176]{0,1:T(8,128)(2,1)S(1)} %copy-done.12), kind=kOutput, calls=%fused_computation.53 | convolution fusion | flops 2955673600 | bytes 12713984 | tf_op jit(solution)/shard_map/dot_general | solution.py:152
  235.7 5.1 %fusion.14 = bf16[2048,2048]{1,0:T(8,128)(2,1)S(1)} fusion(bf16[2048,2048]{1,0:T(8,128)(2,1)S(1)} %bitcast.131, bf16[176,2048]{1,0:T(8,128)(2,1)S(1)} %copy-done, f32[2048]{0:T(1024)S(1)} %get-tuple-element.82, f32[2048,352]{0,1:T(8,128)} %fusion.37), kind=kOutput, calls=%fused_computation.20 | convolution fusion | flops 1495334912 | bytes 20389888 | tf_op jit(solution)/shard_map/dot_general | solution.py:156
  240.8 2.5 dynamic-slice_bitcast_fusion
  243.3 2.0 copy-done.3
  245.5 7.2 %collective-permute-done = bf16[4,2,128,2048]{3,2,1,0:T(8,128)(2,1)} collective-permute-done((bf16[4,2,128,2048]{3,2,1,0:T(8,128)(2,1)}, bf16[4,2,128,2048]{3,2,1,0:T(8,128)(2,1)}, u32[]{:S(2)}, u32[]{:S(2)}) %collective-permute-start) | collective-permute-done | bytes 4194336 | tf_op jit(solution)/shard_map/ppermute | solution.py:68
  252.8 5.4 %convert_add_fusion = f32[4,2,128,2048]{3,2,1,0:T(8,128)S(1)} fusion(bf16[4,2,128,2048]{3,2,1,0:T(8,128)(2,1)} %collective-permute-done, bf16[4,2,2,128,2048]{4,3,2,1,0:T(8,128)(2,1)} %bitcast.130, s32[]{:T(128)S(6)} %select_n.100), kind=kLoop, calls=%fused_computation.22 | loop fusion | flops 6291456 | bytes 16777220 | tf_op jit(solution)/shard_map/add | solution.py:69
  258.2 3.2 fusion.76
  261.4 2.0 copy-done.1
  263.4 1.6 collective-permute-start.1
  265.0 1.3 fusion.61
  266.3 1.8 collective-permute-start.4
  268.1 10.7 %collective-permute-done.1 = bf16[2,128,1024]{2,1,0:T(8,128)(2,1)S(1)} collective-permute-done((bf16[2,128,1024]{2,1,0:T(8,128)(2,1)S(1)}, bf16[2,128,1024]{2,1,0:T(8,128)(2,1)S(1)}, u32[]{:S(2)}, u32[]{:S(2)}) %collective-permute-start.1) | collective-permute-done | bytes 524320 | tf_op jit(solution)/shard_map/ppermute | solution.py:80
  278.8 1.4 fusion.57
  280.5 1.4 fusion.55
  281.9 3.0 collective-permute-start.5
  284.9 9.8 %collective-permute-done.2 = bf16[2,128,1024]{2,1,0:T(8,128)(2,1)S(1)} collective-permute-done((bf16[2,128,1024]{2,1,0:T(8,128)(2,1)S(1)}, bf16[2,128,1024]{2,1,0:T(8,128)(2,1)S(1)}, u32[]{:S(2)}, u32[]{:S(2)}) %collective-permute-start.2) | collective-permute-done | bytes 524320 | tf_op jit(solution)/shard_map/ppermute | solution.py:80
  294.7 1.4 fusion.56
  296.2 1.4 fusion.54
  297.6 3.3 collective-permute-start.6
  300.8 8.9 %collective-permute-done.3 = bf16[2,128,1024]{2,1,0:T(8,128)(2,1)S(1)} collective-permute-done((bf16[2,128,1024]{2,1,0:T(8,128)(2,1)S(1)}, bf16[2,128,1024]{2,1,0:T(8,128)(2,1)S(1)}, u32[]{:S(2)}, u32[]{:S(2)}) %collective-permute-start.3) | collective-permute-done | bytes 524320 | tf_op jit(solution)/shard_map/ppermute | solution.py:80
  309.7 1.4 bitcast_add_fusion.3
  311.1 1.5 bitcast_add_fusion
  312.6 0.9 fusion.62
  313.5 1.3 collective-permute-start.7
  314.8 2.3 maximum_bitcast_fusion
  317.1 1.2 broadcast_in_dim.27
  318.3 3.4 %scatter_fusion = bf16[2,16,128,128]{3,2,1,0:T(8,128)(2,1)} fusion(bf16[2,16,128,128]{3,2,1,0:T(8,128)(2,1)} %broadcast_in_dim.27, s32[16]{0:T(128)S(1)} %compare_select_fusion, bf16[16,2,128,128]{3,2,1,0:T(8,128)(2,1)} %maximum_bitcast_fusion), kind=kCustom, calls=%fused_computation | custom fusion | bytes 3145792 | tf_op jit(solution)/shard_map/scatter | solution.py:134
  321.7 3.5 %collective-permute-done.7 = bf16[128,2048]{1,0:T(8,128)(2,1)} collective-permute-done((bf16[128,2048]{1,0:T(8,128)(2,1)}, bf16[128,2048]{1,0:T(8,128)(2,1)}, u32[]{:S(2)}, u32[]{:S(2)}) %collective-permute-start.7) | collective-permute-done | bytes 524320 | tf_op jit(solution)/shard_map/ppermute | solution.py:96
  325.2 2.0 fusion.48
  (60 shorter events, 3.6 us)
Async XLA Ops:
  7.2 228.5 %copy-start = (bf16[176,2048]{1,0:T(8,128)(2,1)S(1)}, bf16[176,2048]{1,0:T(8,128)(2,1)}, u32[]{:S(2)}) copy-start(bf16[176,2048]{1,0:T(8,128)(2,1)} %param.29) | copy-start | bytes 2162692
  7.2 58.1 %all-gather.4.cloned.1.call-start = ((), (), s32[]{:S(2)}) async-start(), calls=%async_computation.1 | async-start | bytes 8912896 | tf_op jit(solution)/shard_map/all_gather | solution.py:127
  10.6 115.1 %all-gather.6.cloned.1.call-start = ((), (), s32[]{:S(2)}) async-start(), calls=%async_computation.2 | async-start | bytes 8912896 | tf_op jit(solution)/shard_map/all_gather | solution.py:128
  73.6 1.4 copy-start.9
  100.3 25.4 %all-to-all-start = ((bf16[16,128,128]{2,1,0:T(8,128)(2,1)}), bf16[16,128,128]{2,1,0:T(8,128)(2,1)S(1)}, u32[]{:S(2)}, u32[]{:S(2)}) async-start(bf16[16,128,128]{2,1,0:T(8,128)(2,1)} %bitcast.3), calls=%async_computation | async-start | bytes 1048576 | tf_op jit(solution)/shard_map/all_to_all | solution.py:136
  105.2 81.7 %all-gather.8.cloned.1.call-start = ((), (), s32[]{:S(2)}) async-start(), calls=%async_computation.3 | async-start | bytes 8912896 | tf_op jit(solution)/shard_map/all_gather | solution.py:148
  125.7 5.8 %copy-start.4 = (bf16[128,2048]{1,0:T(8,128)(2,1)S(1)}, bf16[128,2048]{1,0:T(8,128)(2,1)}, u32[]{:S(2)}) copy-start(bf16[128,2048]{1,0:T(8,128)(2,1)} %param.19) | copy-start | bytes 1572868
  125.7 6.9 %copy-start.10 = (f32[2048]{0:T(1024)S(1)}, f32[2048]{0:T(1024)}, u32[]{:S(2)}) copy-start(f32[2048]{0:T(1024)} %param.26) | copy-start | bytes 24580
  125.7 8.0 %copy-start.7 = (f32[2048,6]{0,1:T(8,128)S(1)}, f32[2048,6]{0,1:T(8,128)}, u32[]{:S(2)}) copy-start(f32[2048,6]{0,1:T(8,128)} %param.34) | copy-start | bytes 147460
  125.7 8.0 %copy-start.8 = (s32[2048,6]{0,1:T(8,128)S(1)}, s32[2048,6]{0,1:T(8,128)}, u32[]{:S(2)}) copy-start(s32[2048,6]{0,1:T(8,128)} %param.33) | copy-start | bytes 147460
  131.6 62.1 %slice-start = ((s8[5767168]{0:T(1024)(128)(4,1)}), s8[1572864]{0:T(1024)(128)(4,1)S(1)}, s32[]{:S(2)}) async-start(s8[5767168]{0:T(1024)(128)(4,1)} %bitcast.136), calls=%async_computation.4 | async-start | bytes 3145728
  131.8 0.8 copy-start.5
  186.9 6.8 %slice-start.1 = ((s8[5767168]{0:T(1024)(128)(4,1)}), s8[4194304]{0:T(1024)(128)(4,1)S(1)}, s32[]{:S(2)}) async-start(s8[5767168]{0:T(1024)(128)(4,1)} %bitcast.136), calls=%async_computation.5 | async-start | bytes 8388608
  191.7 2.0 copy-start.2
  222.8 4.7 %copy-start.11 = (bf16[2048,176]{0,1:T(8,128)(2,1)S(1)}, bf16[2048,176]{0,1:T(8,128)(2,1)}, u32[]{:S(2)}) copy-start(bf16[2048,176]{0,1:T(8,128)(2,1)} %param.28) | copy-start | bytes 2162692
  222.8 4.7 %copy-start.12 = (bf16[2048,176]{0,1:T(8,128)(2,1)S(1)}, bf16[2048,176]{0,1:T(8,128)(2,1)}, u32[]{:S(2)}) copy-start(bf16[2048,176]{0,1:T(8,128)(2,1)} %param.27) | copy-start | bytes 2162692
  240.8 4.5 %copy-start.3 = (bf16[2048,2048]{1,0:T(8,128)(2,1)}, bf16[2048,2048]{1,0:T(8,128)(2,1)S(1)}, u32[]{:S(2)}) copy-start(bf16[2048,2048]{1,0:T(8,128)(2,1)S(1)} %fusion.14) | copy-start | bytes 25165828
  245.3 7.5 %collective-permute-start = (bf16[4,2,128,2048]{3,2,1,0:T(8,128)(2,1)}, bf16[4,2,128,2048]{3,2,1,0:T(8,128)(2,1)}, u32[]{:S(2)}, u32[]{:S(2)}) collective-permute-start(bf16[4,2,128,2048]{3,2,1,0:T(8,128)(2,1)} %dynamic-slice_bitcast_fusion), channel_id=1, source_target_pairs={{0,1},{1,0},{2,3},{3,2},{4,5},{5,4},{6,7},{7,6},{8,9},{9,8},{10,11... | collective-permute-start | bytes 12582920 | tf_op jit(solution)/shard_map/ppermute | solution.py:68
  261.4 2.0 copy-start.1
  263.4 15.4 %collective-permute-start.1 = (bf16[2,128,1024]{2,1,0:T(8,128)(2,1)S(1)}, bf16[2,128,1024]{2,1,0:T(8,128)(2,1)S(1)}, u32[]{:S(2)}, u32[]{:S(2)}) collective-permute-start(bf16[2,128,1024]{2,1,0:T(8,128)(2,1)S(1)} %fusion.60), channel_id=1, source_target_pairs={{0,4},{1,5},{2,6},{3,7},{4,8},{5,9},{6,10},{7,11},{8,12},{9,13},{1... | collective-permute-start | bytes 1572872 | tf_op jit(solution)/shard_map/ppermute | solution.py:80
  266.3 14.2 %collective-permute-start.4 = (bf16[2,128,1024]{2,1,0:T(8,128)(2,1)S(1)}, bf16[2,128,1024]{2,1,0:T(8,128)(2,1)S(1)}, u32[]{:S(2)}, u32[]{:S(2)}) collective-permute-start(bf16[2,128,1024]{2,1,0:T(8,128)(2,1)S(1)} %fusion.61), channel_id=1, source_target_pairs={{0,12},{1,13},{2,14},{3,15},{4,0},{5,1},{6,2},{7,3},{8,4},{9,5},{1... | collective-permute-start | bytes 1572872 | tf_op jit(solution)/shard_map/ppermute | solution.py:81
  280.1 14.5 %collective-permute-start.2 = (bf16[2,128,1024]{2,1,0:T(8,128)(2,1)S(1)}, bf16[2,128,1024]{2,1,0:T(8,128)(2,1)S(1)}, u32[]{:S(2)}, u32[]{:S(2)}) collective-permute-start(bf16[2,128,1024]{2,1,0:T(8,128)(2,1)S(1)} %fusion.57), channel_id=1, source_target_pairs={{0,4},{1,5},{2,6},{3,7},{4,8},{5,9},{6,10},{7,11},{8,12},{9,13},{1... | collective-permute-start | bytes 1572872 | tf_op jit(solution)/shard_map/ppermute | solution.py:80
  281.9 14.3 %collective-permute-start.5 = (bf16[2,128,1024]{2,1,0:T(8,128)(2,1)S(1)}, bf16[2,128,1024]{2,1,0:T(8,128)(2,1)S(1)}, u32[]{:S(2)}, u32[]{:S(2)}) collective-permute-start(bf16[2,128,1024]{2,1,0:T(8,128)(2,1)S(1)} %fusion.55), channel_id=1, source_target_pairs={{0,12},{1,13},{2,14},{3,15},{4,0},{5,1},{6,2},{7,3},{8,4},{9,5},{1... | collective-permute-start | bytes 1572872 | tf_op jit(solution)/shard_map/ppermute | solution.py:81
  296.1 13.6 %collective-permute-start.3 = (bf16[2,128,1024]{2,1,0:T(8,128)(2,1)S(1)}, bf16[2,128,1024]{2,1,0:T(8,128)(2,1)S(1)}, u32[]{:S(2)}, u32[]{:S(2)}) collective-permute-start(bf16[2,128,1024]{2,1,0:T(8,128)(2,1)S(1)} %fusion.56), channel_id=1, source_target_pairs={{0,4},{1,5},{2,6},{3,7},{4,8},{5,9},{6,10},{7,11},{8,12},{9,13},{1... | collective-permute-start | bytes 1572872 | tf_op jit(solution)/shard_map/ppermute | solution.py:80
  297.5 17.3 %copy-start.13 = (s32[16]{0:T(128)S(1)}, s32[16]{0:T(128)}, u32[]{:S(2)}) copy-start(s32[16]{0:T(128)} %param.35) | copy-start | bytes 196
  297.6 13.5 %collective-permute-start.6 = (bf16[2,128,1024]{2,1,0:T(8,128)(2,1)S(1)}, bf16[2,128,1024]{2,1,0:T(8,128)(2,1)}, u32[]{:S(2)}, u32[]{:S(2)}) collective-permute-start(bf16[2,128,1024]{2,1,0:T(8,128)(2,1)S(1)} %fusion.54), channel_id=1, source_target_pairs={{0,12},{1,13},{2,14},{3,15},{4,0},{5,1},{6,2},{7,3},{8,4},{9,5},{1... | collective-permute-start | bytes 1572872 | tf_op jit(solution)/shard_map/ppermute | solution.py:81
  312.6 12.6 %copy-start.6 = (bf16[128,2048]{1,0:T(8,128)(2,1)S(1)}, bf16[128,2048]{1,0:T(8,128)(2,1)}, u32[]{:S(2)}) copy-start(bf16[128,2048]{1,0:T(8,128)(2,1)} %copy-done.5) | copy-start | bytes 1572868
  313.5 11.7 %collective-permute-start.7 = (bf16[128,2048]{1,0:T(8,128)(2,1)}, bf16[128,2048]{1,0:T(8,128)(2,1)}, u32[]{:S(2)}, u32[]{:S(2)}) collective-permute-start(bf16[128,2048]{1,0:T(8,128)(2,1)} %fusion.62), channel_id=1, source_target_pairs={{0,2},{1,3},{2,0},{3,1},{4,6},{5,7},{6,4},{7,5},{8,10},{9,11},{10,... | collective-permute-start | bytes 1572872 | tf_op jit(solution)/shard_map/ppermute | solution.py:96
Sparse Core Ops, SparseCore 0:
  10.7 54.5 all-gather.3
  67.0 58.6 all-gather.5
  133.8 53.0 all-gather.7

commit v3 on v2

--- a/solution.py
+++ b/solution.py
@@ -145,49 +145,84 @@
     attention = jnp.sum(partials.astype(jnp.float32), axis=0)
     residual = (tokens.astype(jnp.float32) + attention).astype(jnp.bfloat16)
     normed_ffn = rms_scale(residual, ffn_gain)
-    normed_stream = lax.all_gather(normed_ffn, "tensor", axis=0, tiled=True)
-
-    shared_columns = jnp.concatenate([shared_gate, shared_up], axis=1)
-    shared_width = shared_gate.shape[1]
-    joined = jnp.dot(normed_stream, shared_columns, preferred_element_type=jnp.float32)
-    hidden_all = (jax.nn.silu(joined[:, :shared_width]) * joined[:, shared_width:]).astype(
-        jnp.bfloat16
-    )
-    term = jnp.dot(hidden_all, shared_down, preferred_element_type=jnp.float32)
+    pieces = 2
+    piece_width = model_width // pieces
+    stream_pieces = [
+        lax.all_gather(
+            normed_ffn[:, k * piece_width : (k + 1) * piece_width], "tensor", axis=0, tiled=True
+        )
+        for k in range(pieces)
+    ]
 
     local_experts = expert_gate.shape[0]
     expert_count = local_experts * groups
     capacity = tok_dev * TOP // expert_count + tok_dev // 8
     id_blocks = expert_ids.reshape(groups, tok_dev, -1)
     gate_blocks = gate_weights.reshape(groups, tok_dev, -1)
-    token_blocks = normed_stream.reshape(groups, tok_dev, model_width)
     slots = jnp.arange(capacity, dtype=jnp.int32)
+    onehots = []
+    weights = []
     for local in range(local_experts):
         expert = position * local_experts + local
         chosen = id_blocks == expert
         hits = jnp.sum(chosen.astype(jnp.int32), axis=2)
-        weight = jnp.sum(jnp.where(chosen, gate_blocks, 0.0), axis=2)
+        weights.append(jnp.sum(jnp.where(chosen, gate_blocks, 0.0), axis=2))
         rank = jnp.cumsum(hits, axis=1) - hits
-        onehot = ((hits[:, None, :] > 0) & (rank[:, None, :] == slots[None, :, None])).astype(
-            jnp.bfloat16
-        )
-        picked = jnp.einsum(
-            "bst,btd->bsd", onehot, token_blocks, preferred_element_type=jnp.float32
-        ).astype(jnp.bfloat16)
-        rows = expert_apply(
-            picked.reshape(-1, model_width),
-            expert_gate[local],
-            expert_up[local],
-            expert_down[local],
-        )
-        back = jnp.einsum(
-            "bst,bsd->btd",
-            onehot,
-            rows.reshape(groups, capacity, model_width),
-            preferred_element_type=jnp.float32,
-        ).astype(jnp.bfloat16)
-        term = term + weight.reshape(-1, 1) * back.reshape(-1, model_width).astype(jnp.float32)
-    ffn_out = ring_reduce_scatter(term.astype(jnp.bfloat16), groups)
+        onehots.append(
+            ((hits[:, None, :] > 0) & (rank[:, None, :] == slots[None, :, None])).astype(
+                jnp.bfloat16
+            )
+        )
+
+    shared_columns = jnp.concatenate([shared_gate, shared_up], axis=1)
+    shared_width = shared_gate.shape[1]
+    joined = None
+    expert_gate_parts = [None] * local_experts
+    expert_up_parts = [None] * local_experts
+    for k in range(pieces):
+        columns = slice(k * piece_width, (k + 1) * piece_width)
+        piece = stream_pieces[k]
+        step = jnp.dot(piece, shared_columns[columns], preferred_element_type=jnp.float32)
+        joined = step if joined is None else joined + step
+        token_blocks = piece.reshape(groups, tok_dev, piece_width)
+        for local in range(local_experts):
+            picked = jnp.einsum(
+                "bst,btd->bsd", onehots[local], token_blocks, preferred_element_type=jnp.float32
+            ).astype(jnp.bfloat16).reshape(-1, piece_width)
+            g = jnp.dot(picked, expert_gate[local][columns], preferred_element_type=jnp.float32)
+            u = jnp.dot(picked, expert_up[local][columns], preferred_element_type=jnp.float32)
+            if expert_gate_parts[local] is None:
+                expert_gate_parts[local], expert_up_parts[local] = g, u
+            else:
+                expert_gate_parts[local] = expert_gate_parts[local] + g
+                expert_up_parts[local] = expert_up_parts[local] + u
+    hidden_all = (jax.nn.silu(joined[:, :shared_width]) * joined[:, shared_width:]).astype(
+        jnp.bfloat16
+    )
+    expert_hidden = [
+        (jax.nn.silu(expert_gate_parts[local]) * expert_up_parts[local]).astype(jnp.bfloat16)
+        for local in range(local_experts)
+    ]
+
+    outs = []
+    for k in range(pieces):
+        columns = slice(k * piece_width, (k + 1) * piece_width)
+        term = jnp.dot(hidden_all, shared_down[:, columns], preferred_element_type=jnp.float32)
+        for local in range(local_experts):
+            rows = jnp.dot(
+                expert_hidden[local], expert_down[local][:, columns], preferred_element_type=jnp.float32
+            ).astype(jnp.bfloat16)
+            back = jnp.einsum(
+                "bst,bsd->btd",
+                onehots[local],
+                rows.reshape(groups, capacity, piece_width),
+                preferred_element_type=jnp.float32,
+            ).astype(jnp.bfloat16)
+            term = term + weights[local].reshape(-1, 1) * back.reshape(-1, piece_width).astype(
+                jnp.float32
+            )
+        outs.append(ring_reduce_scatter(term.astype(jnp.bfloat16), groups))
+    ffn_out = jnp.concatenate(outs, axis=1)
     layer_out = (residual.astype(jnp.float32) + ffn_out).astype(jnp.bfloat16)
     return (layer_out, kv_pages)
 

time: 335 us -> 338 us (level)
  starting transfers between devices: 16.8 us -> 28.3 us
  waiting for transfers between devices: 168 us -> 158 us
  matrix products: 77.1 us -> 86.2 us
  other arithmetic: 28.9 us -> 21.4 us
  local copies, waits for them, and re-layouts: 22.3 us -> 16.9 us
    all_gather x1 -> x2, waiting for transfers between devices: 52.8 us -> 72.3 us  [shards(): lax.all_gather(normed_ffn[:, k * piece_width:(k + 1) * piece_width], 'ten...]
    ppermute x3 -> x6, waiting for transfers between devices: 29.3 us -> 12.7 us  [ring_reduce_scatter(): recv_f = lax.ppermute(carry_f, 'tensor', forward_pairs)]
    ppermute x3 -> x6, starting transfers between devices: 8.13 us -> 18.4 us  [ring_reduce_scatter(): recv_b = lax.ppermute(carry_b, 'tensor', backward_pairs)]
    dot_general x6 -> x14, matrix products: 51.9 us -> 60.9 us  [the longest x2 13.4 us: shards(): jnp.dot(picked, expert_up[local][columns], preferred_element_type=jnp.flo...]
    ppermute x1 -> x2, waiting for transfers between devices: 7.25 us -> 0.01 us  [ring_reduce_scatter(): got = lax.ppermute(give, 'tensor', core_pairs)]
    unnamed x32 -> x43, local copies, waits for them, and re-layouts: 6.77 us -> 3.02 us
    ppermute x1 -> x2, waiting for transfers between devices: 3.5 us -> 0.01 us  [ring_reduce_scatter(): got_side = lax.ppermute(give_side, 'tensor', side_pairs)]
  transfers between devices with their start and end apart: 12 -> 21, of which waited for: 8 -> 9; matrix products, arithmetic and copies ran while one was open for 13% -> 16% of each run, Pallas kernels for 0% -> 0%
where the time goes in v3:
time: 338 us; the launch traced here: 334 us
  waiting for transfers between devices  158 us (47%)
  matrix products  86.2 us (26%)
  starting transfers between devices  28.3 us (8%)
  other arithmetic  21.4 us (6%)
  local copies, waits for them, and re-layouts  16.9 us (5%)
  between operations  14.6 us (4%)
  loops' own time  8.32 us (2%)
    all_gather x2, waiting for transfers between devices, shards(): lax.all_gather(normed_ffn[:, k * piece_width:(k + 1) * piece_width], 'ten...  72.3 us
    all_gather x1, waiting for transfers between devices, shards(): lax.all_gather(rms_scale(tokens, attention_gain), 'tensor', axis=0, tiled...  53.9 us
    ppermute x6, starting transfers between devices, ring_reduce_scatter(): recv_b = lax.ppermute(carry_b, 'tensor', backward_pairs)  18.4 us
    all_gather x1, waiting for transfers between devices, shards(): out_weight_all = lax.all_gather(output_weight, 'tensor', axis=0, tiled=True)  17.9 us
    dot_general x2, matrix products, shards(): jnp.dot(picked, expert_up[local][columns], preferred_element_type=jnp.flo...  13.4 us
    dot_general x2, matrix products, shards(): jnp.dot(hidden_all, shared_down[:, columns], preferred_element_type=jnp.f...  13.3 us
    ppermute x6, waiting for transfers between devices, ring_reduce_scatter(): recv_f = lax.ppermute(carry_f, 'tensor', forward_pairs)  12.7 us
    dot_general x2, matrix products, shards(): jnp.dot(picked, expert_gate[local][columns], preferred_element_type=jnp.f...  12.6 us
  transfers between devices with their start and end apart: 21, of which 9 were waited for; matrix products, arithmetic and copies ran while one was open for 16% of the time, Pallas kernels for 0%

profile of v3, /device:TPU:0, one launch (start us, length us, event | category | flops | bytes accessed | tf_op | source)
XLA Modules:
  0.0 333.7 jit_solution(5062776784792137415)
XLA Ops:
  7.2 1.2 fusion.44
  8.4 2.0 fusion.46
  11.3 53.9 %all-gather.5.cloned.1.call-done = bf16[2048,2048]{1,0:T(8,128)(2,1)} async-done(((bf16[128,2048]{1,0:T(8,128)(2,1)}), bf16[2048,2048]{1,0:T(8,128)(2,1)}) %all-gather.5.cloned.1.call-update) | async-done | bytes 8388624 | tf_op jit(solution)/shard_map/all_gather | solution.py:127
  65.2 8.3 %convolution_convert_fusion = bf16[2048,384]{1,0:T(8,128)(2,1)S(1)} fusion(bf16[2048,2048]{1,0:T(8,128)(2,1)} %all-gather.5.cloned.1.call-done, bf16[2048,128]{1,0:T(8,128)(2,1)} %param.24, bf16[2048,128]{1,0:T(8,128)(2,1)} %param.23, bf16[2048,128]{1,0:T(8,128)(2,1)} %param.22), kind=kOutput, calls=%fused_computation.43 | convolution fusion | flops 3226730496 | bytes 11534336 | tf_op jit(solution)/shard_map/dot_general | solution.py:129
  73.5 1.2 fusion.99
  74.6 28.1 %while.11 = (s32[]{:T(128)}, bf16[4,512,1,128]{3,1,2,0:T(8,128)(2,1)}, s32[4]{0:T(128)S(1)}, s32[2048]{0:T(1024)S(1)}, bf16[2048,1,128]{2,0,1:T(8,128)(2,1)S(1)}...) while((s32[]{:T(128)}, ...), condition=%wide.region_4.5_spmd.clone, body=%wide.region_1.4_spmd.clone.sunk | while | flops 548470272 | bytes 13922475 | solution.py:45
  78.2 1.3 fusion.123
  79.4 0.7 fusion.124
  80.1 1.5 fusion.125
  85.2 1.3 fusion.123
  86.5 0.7 fusion.124
  87.2 1.5 fusion.125
  92.2 1.3 fusion.123
  93.5 0.7 fusion.124
  94.2 1.5 fusion.125
  99.2 1.3 fusion.123
  101.2 1.5 fusion.125
  102.8 4.9 %all-to-all-start = ((bf16[16,128,128]{2,1,0:T(8,128)(2,1)}), bf16[16,128,128]{2,1,0:T(8,128)(2,1)S(1)}, u32[]{:S(2)}, u32[]{:S(2)}) async-start(bf16[16,128,128]{2,1,0:T(8,128)(2,1)} %bitcast.3), calls=%async_computation | async-start | bytes 1048576 | tf_op jit(solution)/shard_map/all_to_all | solution.py:136
  107.7 17.9 %all-gather.7.cloned.1.call-done = bf16[2048,2048]{1,0:T(8,128)(2,1)} async-done(((bf16[128,2048]{1,0:T(8,128)(2,1)}), bf16[2048,2048]{1,0:T(8,128)(2,1)}) %all-gather.7.cloned.1.call-update) | async-done | bytes 8388624 | tf_op jit(solution)/shard_map/all_gather | solution.py:128
  125.6 5.8 %convert_reduce_fusion = f32[128,2048]{1,0:T(8,128)S(1)} fusion(bf16[16,128,128]{2,1,0:T(8,128)(2,1)S(1)} %all-to-all-done, bf16[16,128,2048]{2,1,0:T(8,128)(2,1)} %bitcast.170), kind=kOutput, calls=%fused_computation.18 | convolution fusion | flops 1086062592 | bytes 9961472 | tf_op jit(solution)/shard_map/gtd,gdo->gto/dot_general | solution.py:139
  131.9 0.8 fusion.100
  133.8 0.9 constant_dynamic-update-slice_fusion.1
  134.7 0.9 constant_dynamic-update-slice_fusion
  135.6 35.7 %all-gather.9.cloned.1.call-done = bf16[2048,1024]{1,0:T(8,128)(2,1)} async-done(((bf16[128,1024]{1,0:T(8,128)(2,1)}), bf16[2048,1024]{1,0:T(8,128)(2,1)}) %all-gather.9.cloned.1.call-update) | async-done | bytes 4194320 | tf_op jit(solution)/shard_map/all_gather | solution.py:151
  171.3 2.9 convolution_convert_fusion.4
  174.2 36.7 %all-gather.11.cloned.1.call-done = bf16[2048,1024]{1,0:T(8,128)(2,1)} async-done(((bf16[128,1024]{1,0:T(8,128)(2,1)}), bf16[2048,1024]{1,0:T(8,128)(2,1)}) %all-gather.11.cloned.1.call-update) | async-done | bytes 4194320 | tf_op jit(solution)/shard_map/all_gather | solution.py:151
  210.8 3.0 convolution_convert_fusion.3
  213.9 7.4 %fusion.24 = f32[1024,1408]{1,0:T(8,128)} fusion(bf16[1024,1024]{1,0:T(8,128)(2,1)S(1)} %bitcast.183, bf16[1,2048,1408]{2,1,0:T(8,128)(2,1)} %param.30), kind=kOutput, calls=%fused_computation.35 | convolution fusion | flops 2952790016 | bytes 10747904 | tf_op jit(solution)/shard_map/dot_general | solution.py:192
  221.3 5.2 %fusion.26 = f32[1024,1408]{1,0:T(8,128)} fusion(bf16[1024,1024]{1,0:T(8,128)(2,1)S(1)} %bitcast.181, bf16[1,2048,1408]{2,1,0:T(8,128)(2,1)S(1)} %bitcast.189), kind=kOutput, calls=%fused_computation.37 | convolution fusion | flops 2952790016 | bytes 10747904 | tf_op jit(solution)/shard_map/dot_general | solution.py:192
  226.5 5.2 %fusion.22 = f32[1024,1408]{1,0:T(8,128)} fusion(bf16[1024,1024]{1,0:T(8,128)(2,1)S(1)} %bitcast.182, bf16[1,2048,1408]{2,1,0:T(8,128)(2,1)S(1)} %bitcast.191), kind=kOutput, calls=%fused_computation.33 | convolution fusion | flops 2952790016 | bytes 10747904 | tf_op jit(solution)/shard_map/dot_general | solution.py:193
  231.8 8.2 %multiply_convert_fusion = bf16[1024,1408]{1,0:T(8,128)(2,1)S(1)} fusion(f32[1024,1408]{1,0:T(8,128)} %fusion.22, f32[1024,1408]{1,0:T(8,128)} %fusion.26, f32[1024,1408]{1,0:T(8,128)} %fusion.24, bf16[1024,1024]{1,0:T(8,128)(2,1)S(1)} %bitcast.184, bf16[1,2048,1408]{2,1,0:T(8,128)(2,1)S(1)} %bitcast.191), kind=kOutput, calls=%fused_computation.25 | convolution fusion | flops 2964324352 | bytes 25165824 | tf_op jit(solution)/shard_map/dot_general | solution.py:193
  240.0 3.6 %fusion.35 = bf16[1024,1024]{1,0:T(8,128)(2,1)S(1)} fusion(bf16[1024,1408]{1,0:T(8,128)(2,1)S(1)} %multiply_convert_fusion, bf16[1408,2048]{1,0:T(8,128)(2,1)S(1)} %bitcast.194), kind=kOutput, calls=%fused_computation.50 | convolution fusion | flops 2953838592 | bytes 7864320 | tf_op jit(solution)/shard_map/dot_general | solution.py:212
  243.6 3.6 %fusion.32 = bf16[1024,1024]{1,0:T(8,128)(2,1)S(1)} fusion(bf16[1024,1408]{1,0:T(8,128)(2,1)S(1)} %multiply_convert_fusion, bf16[1408,2048]{1,0:T(8,128)(2,1)S(1)} %bitcast.195), kind=kOutput, calls=%fused_computation.49 | convolution fusion | flops 2953838592 | bytes 7864320 | tf_op jit(solution)/shard_map/dot_general | solution.py:212
  247.3 3.0 fusion.53
  250.3 2.8 convolution_add_fusion
  253.6 1.3 convolution_convert_fusion.1
  254.9 11.6 %fusion.14 = bf16[2048,1024]{1,0:T(8,128)(2,1)S(1)} fusion(bf16[2048,1024]{1,0:T(8,128)(2,1)S(1)} %bitcast.174, bf16[2048,176]{0,1:T(8,128)(2,1)S(1)} %fusion.43, f32[2048]{0:T(1024)S(1)} %get-tuple-element.82, bf16[176,2048]{1,0:T(8,128)(2,1)S(1)} %copy-done.13), kind=kOutput, calls=%fused_computation.21 | convolution fusion | flops 746586112 | bytes 9478144 | tf_op jit(solution)/shard_map/dot_general | solution.py:210
  266.5 1.8 dynamic-slice_bitcast_fusion
  268.6 1.3 convolution_convert_fusion.2
  269.9 1.7 fusion.16
  271.6 2.0 copy-done.3
  274.1 3.2 convert_add_fusion
  278.0 1.3 collective-permute-start.9
  279.3 2.1 collective-permute-start.12
  281.4 2.5 convert_add_fusion.1
  284.7 3.2 collective-permute-start.4
  288.3 3.2 collective-permute-start.13
  291.5 3.7 %collective-permute-done.1 = bf16[2,128,512]{2,1,0:T(8,128)(2,1)S(1)} collective-permute-done((bf16[2,128,512]{2,1,0:T(8,128)(2,1)S(1)}, bf16[2,128,512]{2,1,0:T(8,128)(2,1)S(1)}, u32[]{:S(2)}, u32[]{:S(2)}) %collective-permute-start.1) | collective-permute-done | bytes 262176 | tf_op jit(solution)/shard_map/ppermute | solution.py:80
  295.4 3.3 collective-permute-start.5
  298.7 2.1 collective-permute-done.10
  301.0 3.3 collective-permute-start.14
  304.3 2.1 collective-permute-done.2
  306.6 3.3 collective-permute-start.6
  309.9 2.1 collective-permute-done.11
  312.2 1.3 collective-permute-start.15
  313.5 2.8 collective-permute-done.3
  316.5 0.7 fusion.84
  317.2 1.2 collective-permute-start.7
  318.4 1.1 maximum_bitcast_fusion
  319.5 1.2 broadcast_in_dim.27
  320.7 3.4 %scatter_fusion = bf16[2,16,128,128]{3,2,1,0:T(8,128)(2,1)} fusion(bf16[2,16,128,128]{3,2,1,0:T(8,128)(2,1)} %broadcast_in_dim.27, s32[16]{0:T(128)S(1)} %compare_select_fusion, bf16[16,2,128,128]{3,2,1,0:T(8,128)(2,1)} %maximum_bitcast_fusion), kind=kCustom, calls=%fused_computation | custom fusion | bytes 3145792 | tf_op jit(solution)/shard_map/scatter | solution.py:134
  324.1 1.0 fusion.59
  325.1 1.0 fusion.64
  326.1 0.9 fusion.51
  (117 shorter events, 12.8 us)
Async XLA Ops:
  7.2 58.1 %all-gather.5.cloned.1.call-start = ((), (), s32[]{:S(2)}) async-start(), calls=%async_computation.1 | async-start | bytes 8912896 | tf_op jit(solution)/shard_map/all_gather | solution.py:127
  10.5 115.1 %all-gather.7.cloned.1.call-start = ((), (), s32[]{:S(2)}) async-start(), calls=%async_computation.2 | async-start | bytes 8912896 | tf_op jit(solution)/shard_map/all_gather | solution.py:128
  73.5 1.2 copy-start.11
  102.8 22.8 %all-to-all-start = ((bf16[16,128,128]{2,1,0:T(8,128)(2,1)}), bf16[16,128,128]{2,1,0:T(8,128)(2,1)S(1)}, u32[]{:S(2)}, u32[]{:S(2)}) async-start(bf16[16,128,128]{2,1,0:T(8,128)(2,1)} %bitcast.3), calls=%async_computation | async-start | bytes 1048576 | tf_op jit(solution)/shard_map/all_to_all | solution.py:136
  107.7 63.6 %all-gather.9.cloned.1.call-start = ((), (), s32[]{:S(2)}) async-start(), calls=%async_computation.3 | async-start | bytes 4456448 | tf_op jit(solution)/shard_map/all_gather | solution.py:151
  125.6 5.8 %copy-start = (bf16[128,2048]{1,0:T(8,128)(2,1)S(1)}, bf16[128,2048]{1,0:T(8,128)(2,1)}, u32[]{:S(2)}) copy-start(bf16[128,2048]{1,0:T(8,128)(2,1)} %param.19) | copy-start | bytes 1572868
  125.6 6.1 %copy-start.12 = (f32[2048]{0:T(1024)S(1)}, f32[2048]{0:T(1024)}, u32[]{:S(2)}) copy-start(f32[2048]{0:T(1024)} %param.26) | copy-start | bytes 24580
  131.4 1.9 copy-start.9
  131.4 1.9 copy-start.10
  131.4 2.3 copy-start.7
  131.5 3.2 copy-start.8
  132.8 78.1 %all-gather.11.cloned.1.call-start = ((), (), s32[]{:S(2)}) async-start(), calls=%async_computation.4 | async-start | bytes 4456448 | tf_op jit(solution)/shard_map/all_gather | solution.py:151
  210.8 10.5 %slice-start = ((s8[5767168]{0:T(1024)(128)(4,1)}), s8[4194304]{0:T(1024)(128)(4,1)S(1)}, s32[]{:S(2)}) async-start(s8[5767168]{0:T(1024)(128)(4,1)} %bitcast.188), calls=%async_computation.5 | async-start | bytes 8388608
  213.9 7.4 %slice-start.1 = ((s8[5767168]{0:T(1024)(128)(4,1)}), s8[1572864]{0:T(1024)(128)(4,1)S(1)}, s32[]{:S(2)}) async-start(s8[5767168]{0:T(1024)(128)(4,1)} %bitcast.188), calls=%async_computation.6 | async-start | bytes 3145728
  213.9 12.6 %slice-start.2 = ((s8[5767168]{0:T(1024)(128)(4,1)}), s8[4194304]{0:T(1024)(128)(4,1)S(1)}, s32[]{:S(2)}) async-start(s8[5767168]{0:T(1024)(128)(4,1)} %bitcast.190), calls=%async_computation.7 | async-start | bytes 8388608
  221.3 5.2 %slice-start.3 = ((s8[5767168]{0:T(1024)(128)(4,1)}), s8[1572864]{0:T(1024)(128)(4,1)S(1)}, s32[]{:S(2)}) async-start(s8[5767168]{0:T(1024)(128)(4,1)} %bitcast.190), calls=%async_computation.8 | async-start | bytes 3145728
  226.5 13.4 %slice-start.4 = ((s8[5767168]{0:T(1024)(128)(4,1)}), s8[4194304]{0:T(1024)(128)(4,1)S(1)}, s32[]{:S(2)}) async-start(s8[5767168]{0:T(1024)(128)(4,1)} %bitcast.192), calls=%async_computation.9 | async-start | bytes 8388608
  231.7 8.2 %slice-start.5 = ((s8[5767168]{0:T(1024)(128)(4,1)}), s8[1572864]{0:T(1024)(128)(4,1)S(1)}, s32[]{:S(2)}) async-start(s8[5767168]{0:T(1024)(128)(4,1)} %bitcast.192), calls=%async_computation.10 | async-start | bytes 3145728
  243.6 3.7 %copy-start.1 = (bf16[2048,1024]{1,0:T(8,128)(2,1)S(1)}, bf16[2048,1024]{1,0:T(8,128)(2,1)}, u32[]{:S(2)}) copy-start(bf16[2048,1024]{1,0:T(8,128)(2,1)} %all-gather.9.cloned.1.call-done) | copy-start | bytes 12582916
  247.3 3.0 copy-start.2
  253.5 1.3 copy-start.13
  266.5 3.4 %copy-start.5 = (bf16[2048,1024]{1,0:T(8,128)(2,1)}, bf16[2048,1024]{1,0:T(8,128)(2,1)S(1)}, u32[]{:S(2)}) copy-start(bf16[2048,1024]{1,0:T(8,128)(2,1)S(1)} %fusion.14) | copy-start | bytes 12582916
  268.3 5.8 %collective-permute-start.8 = (bf16[4,2,128,1024]{3,2,1,0:T(8,128)(2,1)}, bf16[4,2,128,1024]{3,2,1,0:T(8,128)(2,1)}, u32[]{:S(2)}, u32[]{:S(2)}) collective-permute-start(bf16[4,2,128,1024]{3,2,1,0:T(8,128)(2,1)} %dynamic-slice_bitcast_fusion), channel_id=1, source_target_pairs={{0,1},{1,0},{2,3},{3,2},{4,5},{5,4},{6,7},{7,6},{8,9},{9,8},{10,11... | collective-permute-start | bytes 6291464 | tf_op jit(solution)/shard_map/ppermute | solution.py:68
  271.6 2.0 copy-start.3
  271.6 2.5 copy-start.14
  273.8 7.6 %collective-permute-start = (bf16[4,2,128,1024]{3,2,1,0:T(8,128)(2,1)S(1)}, bf16[4,2,128,1024]{3,2,1,0:T(8,128)(2,1)}, u32[]{:S(2)}, u32[]{:S(2)}) collective-permute-start(bf16[4,2,128,1024]{3,2,1,0:T(8,128)(2,1)S(1)} %dynamic-slice_bitcast_fusion.1), channel_id=1, source_target_pairs={{0,1},{1,0},{2,3},{3,2},{4,5},{5,4},{6,7},{7,6},{8,9},{9,8},{10,11... | collective-permute-start | bytes 6291464 | tf_op jit(solution)/shard_map/ppermute | solution.py:68
  277.3 4.1 %copy-start.4 = (bf16[2048,1024]{1,0:T(8,128)(2,1)S(1)}, bf16[2048,1024]{1,0:T(8,128)(2,1)}, u32[]{:S(2)}) copy-start(bf16[2048,1024]{1,0:T(8,128)(2,1)} %copy-done.3) | copy-start | bytes 12582916
  278.0 10.0 %collective-permute-start.9 = (bf16[2,128,512]{2,1,0:T(8,128)(2,1)S(1)}, bf16[2,128,512]{2,1,0:T(8,128)(2,1)S(1)}, u32[]{:S(2)}, u32[]{:S(2)}) collective-permute-start(bf16[2,128,512]{2,1,0:T(8,128)(2,1)S(1)} %fusion.82), channel_id=1, source_target_pairs={{0,4},{1,5},{2,6},{3,7},{4,8},{5,9},{6,10},{7,11},{8,12},{9,13},{1... | collective-permute-start | bytes 786440 | tf_op jit(solution)/shard_map/ppermute | solution.py:80
  279.3 8.9 %collective-permute-start.12 = (bf16[2,128,512]{2,1,0:T(8,128)(2,1)S(1)}, bf16[2,128,512]{2,1,0:T(8,128)(2,1)S(1)}, u32[]{:S(2)}, u32[]{:S(2)}) collective-permute-start(bf16[2,128,512]{2,1,0:T(8,128)(2,1)S(1)} %fusion.83), channel_id=1, source_target_pairs={{0,12},{1,13},{2,14},{3,15},{4,0},{5,1},{6,2},{7,3},{8,4},{9,5},{1... | collective-permute-start | bytes 786440 | tf_op jit(solution)/shard_map/ppermute | solution.py:81
  284.6 10.5 %collective-permute-start.1 = (bf16[2,128,512]{2,1,0:T(8,128)(2,1)S(1)}, bf16[2,128,512]{2,1,0:T(8,128)(2,1)S(1)}, u32[]{:S(2)}, u32[]{:S(2)}) collective-permute-start(bf16[2,128,512]{2,1,0:T(8,128)(2,1)S(1)} %fusion.80), channel_id=1, source_target_pairs={{0,4},{1,5},{2,6},{3,7},{4,8},{5,9},{6,10},{7,11},{8,12},{9,13},{1... | collective-permute-start | bytes 786440 | tf_op jit(solution)/shard_map/ppermute | solution.py:80
  284.7 10.6 %collective-permute-start.4 = (bf16[2,128,512]{2,1,0:T(8,128)(2,1)S(1)}, bf16[2,128,512]{2,1,0:T(8,128)(2,1)S(1)}, u32[]{:S(2)}, u32[]{:S(2)}) collective-permute-start(bf16[2,128,512]{2,1,0:T(8,128)(2,1)S(1)} %fusion.81), channel_id=1, source_target_pairs={{0,12},{1,13},{2,14},{3,15},{4,0},{5,1},{6,2},{7,3},{8,4},{9,5},{1... | collective-permute-start | bytes 786440 | tf_op jit(solution)/shard_map/ppermute | solution.py:81
  288.0 12.7 %collective-permute-start.10 = (bf16[2,128,512]{2,1,0:T(8,128)(2,1)S(1)}, bf16[2,128,512]{2,1,0:T(8,128)(2,1)S(1)}, u32[]{:S(2)}, u32[]{:S(2)}) collective-permute-start(bf16[2,128,512]{2,1,0:T(8,128)(2,1)S(1)} %fusion.68), channel_id=1, source_target_pairs={{0,4},{1,5},{2,6},{3,7},{4,8},{5,9},{6,10},{7,11},{8,12},{9,13},{1... | collective-permute-start | bytes 786440 | tf_op jit(solution)/shard_map/ppermute | solution.py:80
  288.3 12.7 %collective-permute-start.13 = (bf16[2,128,512]{2,1,0:T(8,128)(2,1)S(1)}, bf16[2,128,512]{2,1,0:T(8,128)(2,1)S(1)}, u32[]{:S(2)}, u32[]{:S(2)}) collective-permute-start(bf16[2,128,512]{2,1,0:T(8,128)(2,1)S(1)} %fusion.66), channel_id=1, source_target_pairs={{0,12},{1,13},{2,14},{3,15},{4,0},{5,1},{6,2},{7,3},{8,4},{9,5},{1... | collective-permute-start | bytes 786440 | tf_op jit(solution)/shard_map/ppermute | solution.py:81
  295.2 11.2 %collective-permute-start.2 = (bf16[2,128,512]{2,1,0:T(8,128)(2,1)S(1)}, bf16[2,128,512]{2,1,0:T(8,128)(2,1)S(1)}, u32[]{:S(2)}, u32[]{:S(2)}) collective-permute-start(bf16[2,128,512]{2,1,0:T(8,128)(2,1)S(1)} %fusion.72), channel_id=1, source_target_pairs={{0,4},{1,5},{2,6},{3,7},{4,8},{5,9},{6,10},{7,11},{8,12},{9,13},{1... | collective-permute-start | bytes 786440 | tf_op jit(solution)/shard_map/ppermute | solution.py:80
  295.4 11.1 %collective-permute-start.5 = (bf16[2,128,512]{2,1,0:T(8,128)(2,1)S(1)}, bf16[2,128,512]{2,1,0:T(8,128)(2,1)S(1)}, u32[]{:S(2)}, u32[]{:S(2)}) collective-permute-start(bf16[2,128,512]{2,1,0:T(8,128)(2,1)S(1)} %fusion.70), channel_id=1, source_target_pairs={{0,12},{1,13},{2,14},{3,15},{4,0},{5,1},{6,2},{7,3},{8,4},{9,5},{1... | collective-permute-start | bytes 786440 | tf_op jit(solution)/shard_map/ppermute | solution.py:81
  300.8 11.2 %collective-permute-start.11 = (bf16[2,128,512]{2,1,0:T(8,128)(2,1)S(1)}, bf16[2,128,512]{2,1,0:T(8,128)(2,1)S(1)}, u32[]{:S(2)}, u32[]{:S(2)}) collective-permute-start(bf16[2,128,512]{2,1,0:T(8,128)(2,1)S(1)} %fusion.67), channel_id=1, source_target_pairs={{0,4},{1,5},{2,6},{3,7},{4,8},{5,9},{6,10},{7,11},{8,12},{9,13},{1... | collective-permute-start | bytes 786440 | tf_op jit(solution)/shard_map/ppermute | solution.py:80
  301.0 11.1 %collective-permute-start.14 = (bf16[2,128,512]{2,1,0:T(8,128)(2,1)S(1)}, bf16[2,128,512]{2,1,0:T(8,128)(2,1)S(1)}, u32[]{:S(2)}, u32[]{:S(2)}) collective-permute-start(bf16[2,128,512]{2,1,0:T(8,128)(2,1)S(1)} %fusion.65), channel_id=1, source_target_pairs={{0,12},{1,13},{2,14},{3,15},{4,0},{5,1},{6,2},{7,3},{8,4},{9,5},{1... | collective-permute-start | bytes 786440 | tf_op jit(solution)/shard_map/ppermute | solution.py:81
  306.4 9.8 %collective-permute-start.3 = (bf16[2,128,512]{2,1,0:T(8,128)(2,1)S(1)}, bf16[2,128,512]{2,1,0:T(8,128)(2,1)S(1)}, u32[]{:S(2)}, u32[]{:S(2)}) collective-permute-start(bf16[2,128,512]{2,1,0:T(8,128)(2,1)S(1)} %fusion.71), channel_id=1, source_target_pairs={{0,4},{1,5},{2,6},{3,7},{4,8},{5,9},{6,10},{7,11},{8,12},{9,13},{1... | collective-permute-start | bytes 786440 | tf_op jit(solution)/shard_map/ppermute | solution.py:80
  306.6 9.7 %collective-permute-start.6 = (bf16[2,128,512]{2,1,0:T(8,128)(2,1)S(1)}, bf16[2,128,512]{2,1,0:T(8,128)(2,1)S(1)}, u32[]{:S(2)}, u32[]{:S(2)}) collective-permute-start(bf16[2,128,512]{2,1,0:T(8,128)(2,1)S(1)} %fusion.69), channel_id=1, source_target_pairs={{0,12},{1,13},{2,14},{3,15},{4,0},{5,1},{6,2},{7,3},{8,4},{9,5},{1... | collective-permute-start | bytes 786440 | tf_op jit(solution)/shard_map/ppermute | solution.py:81
  312.1 6.3 %copy-start.6 = (bf16[2048,128]{1,0:T(8,128)(2,1)S(1)}, bf16[2048,128]{1,0:T(8,128)(2,1)}, u32[]{:S(2)}) copy-start(bf16[2048,128]{1,0:T(8,128)(2,1)} %get-tuple-element.95) | copy-start | bytes 1572868
  312.2 11.9 %collective-permute-start.15 = (bf16[128,1024]{1,0:T(8,128)(2,1)S(1)}, bf16[128,1024]{1,0:T(8,128)(2,1)}, u32[]{:S(2)}, u32[]{:S(2)}) collective-permute-start(bf16[128,1024]{1,0:T(8,128)(2,1)S(1)} %fusion.85), channel_id=1, source_target_pairs={{0,2},{1,3},{2,0},{3,1},{4,6},{5,7},{6,4},{7,5},{8,10},{9,11},{10,... | collective-permute-start | bytes 786440 | tf_op jit(solution)/shard_map/ppermute | solution.py:96
  317.2 7.9 %collective-permute-start.7 = (bf16[128,1024]{1,0:T(8,128)(2,1)}, bf16[128,1024]{1,0:T(8,128)(2,1)}, u32[]{:S(2)}, u32[]{:S(2)}) collective-permute-start(bf16[128,1024]{1,0:T(8,128)(2,1)} %fusion.84), channel_id=1, source_target_pairs={{0,2},{1,3},{2,0},{3,1},{4,6},{5,7},{6,4},{7,5},{8,10},{9,11},{10,... | collective-permute-start | bytes 786440 | tf_op jit(solution)/shard_map/ppermute | solution.py:96
Sparse Core Ops, SparseCore 0:
  10.6 54.5 all-gather.4
  66.9 58.6 all-gather.6
  132.9 38.3 all-gather.8
  173.4 37.3 all-gather.10

commit v4 on v3

--- a/solution.py
+++ b/solution.py
@@ -147,12 +147,7 @@
     normed_ffn = rms_scale(residual, ffn_gain)
     pieces = 2
     piece_width = model_width // pieces
-    stream_pieces = [
-        lax.all_gather(
-            normed_ffn[:, k * piece_width : (k + 1) * piece_width], "tensor", axis=0, tiled=True
-        )
-        for k in range(pieces)
-    ]
+    normed_stream = lax.all_gather(normed_ffn, "tensor", axis=0, tiled=True)
 
     local_experts = expert_gate.shape[0]
     expert_count = local_experts * groups
@@ -176,26 +171,18 @@
 
     shared_columns = jnp.concatenate([shared_gate, shared_up], axis=1)
     shared_width = shared_gate.shape[1]
-    joined = None
-    expert_gate_parts = [None] * local_experts
-    expert_up_parts = [None] * local_experts
-    for k in range(pieces):
-        columns = slice(k * piece_width, (k + 1) * piece_width)
-        piece = stream_pieces[k]
-        step = jnp.dot(piece, shared_columns[columns], preferred_element_type=jnp.float32)
-        joined = step if joined is None else joined + step
-        token_blocks = piece.reshape(groups, tok_dev, piece_width)
-        for local in range(local_experts):
-            picked = jnp.einsum(
-                "bst,btd->bsd", onehots[local], token_blocks, preferred_element_type=jnp.float32
-            ).astype(jnp.bfloat16).reshape(-1, piece_width)
-            g = jnp.dot(picked, expert_gate[local][columns], preferred_element_type=jnp.float32)
-            u = jnp.dot(picked, expert_up[local][columns], preferred_element_type=jnp.float32)
-            if expert_gate_parts[local] is None:
-                expert_gate_parts[local], expert_up_parts[local] = g, u
-            else:
-                expert_gate_parts[local] = expert_gate_parts[local] + g
-                expert_up_parts[local] = expert_up_parts[local] + u
+    joined = jnp.dot(normed_stream, shared_columns, preferred_element_type=jnp.float32)
+    token_blocks = normed_stream.reshape(groups, tok_dev, model_width)
+    expert_gate_parts = []
+    expert_up_parts = []
+    for local in range(local_experts):
+        picked = jnp.einsum(
+            "bst,btd->bsd", onehots[local], token_blocks, preferred_element_type=jnp.float32
+        ).astype(jnp.bfloat16).reshape(-1, model_width)
+        expert_gate_parts.append(
+            jnp.dot(picked, expert_gate[local], preferred_element_type=jnp.float32)
+        )
+        expert_up_parts.append(jnp.dot(picked, expert_up[local], preferred_element_type=jnp.float32))
     hidden_all = (jax.nn.silu(joined[:, :shared_width]) * joined[:, shared_width:]).astype(
         jnp.bfloat16
     )

time: 338 us -> 303 us (0.90)
  waiting for transfers between devices: 158 us -> 140 us
  matrix products: 86.2 us -> 73.1 us
    all_gather x2 -> x1, waiting for transfers between devices: 72.3 us -> 52.8 us  [shards(): normed_stream = lax.all_gather(normed_ffn, 'tensor', axis=0, tiled=True)]
    dot_general x6 -> x3, matrix products: 31.8 us -> 19.8 us  [the longest x1 9.61 us: shards(): jnp.dot(picked, expert_gate[local], preferred_element_type=jnp.float32)]
  transfers between devices with their start and end apart: 21 -> 20, of which waited for: 9 -> 8; matrix products, arithmetic and copies ran while one was open for 16% -> 16% of each run, Pallas kernels for 0% -> 0%
where the time goes in v4:
time: 303 us; the launch traced here: 299 us
  waiting for transfers between devices  140 us (46%)
  matrix products  73.1 us (24%)
  starting transfers between devices  28.6 us (9%)
  other arithmetic  21.7 us (7%)
  between operations  14.6 us (5%)
  local copies, waits for them, and re-layouts  13.9 us (5%)
  loops' own time  6.9 us (2%)
    all_gather x1, waiting for transfers between devices, shards(): lax.all_gather(rms_scale(tokens, attention_gain), 'tensor', axis=0, tiled...  53.9 us
    all_gather x1, waiting for transfers between devices, shards(): normed_stream = lax.all_gather(normed_ffn, 'tensor', axis=0, tiled=True)  52.8 us
    all_gather x1, waiting for transfers between devices, shards(): out_weight_all = lax.all_gather(output_weight, 'tensor', axis=0, tiled=True)  20.1 us
    ppermute x6, starting transfers between devices, ring_reduce_scatter(): recv_b = lax.ppermute(carry_b, 'tensor', backward_pairs)  17.2 us
    dot_general x2, matrix products, shards(): jnp.dot(hidden_all, shared_down[:, columns], preferred_element_type=jnp.f...  13.3 us
    ppermute x6, waiting for transfers between devices, ring_reduce_scatter(): recv_f = lax.ppermute(carry_f, 'tensor', forward_pairs)  12.5 us
    dot_general x1, matrix products, shards(): jnp.dot(picked, expert_gate[local], preferred_element_type=jnp.float32)  9.61 us
    dot_general x1, matrix products, shards(): jnp.dot(normed_all, projection, preferred_element_type=jnp.float32)  8.26 us
  transfers between devices with their start and end apart: 20, of which 8 were waited for; matrix products, arithmetic and copies ran while one was open for 16% of the time, Pallas kernels for 0%

profile of v4, /device:TPU:0, one launch (start us, length us, event | category | flops | bytes accessed | tf_op | source)
XLA Modules:
  0.0 298.9 jit_solution(1911348010598416525)
XLA Ops:
  7.2 1.2 fusion.43
  8.4 2.0 fusion.45
  10.6 0.7 all-gather.6.cloned.1.call-update
  11.3 53.9 %all-gather.4.cloned.1.call-done = bf16[2048,2048]{1,0:T(8,128)(2,1)} async-done(((bf16[128,2048]{1,0:T(8,128)(2,1)}), bf16[2048,2048]{1,0:T(8,128)(2,1)}) %all-gather.4.cloned.1.call-update) | async-done | bytes 8388624 | tf_op jit(solution)/shard_map/all_gather | solution.py:127
  65.2 8.3 %convolution_convert_fusion.1 = bf16[2048,384]{1,0:T(8,128)(2,1)S(1)} fusion(bf16[2048,2048]{1,0:T(8,128)(2,1)} %all-gather.4.cloned.1.call-done, bf16[2048,128]{1,0:T(8,128)(2,1)} %param.24, bf16[2048,128]{1,0:T(8,128)(2,1)} %param.23, bf16[2048,128]{1,0:T(8,128)(2,1)} %param.22), kind=kOutput, calls=%fused_computation.37 | convolution fusion | flops 3226730496 | bytes 11534336 | tf_op jit(solution)/shard_map/dot_general | solution.py:129
  73.5 1.2 fusion.93
  74.6 25.9 %while.11 = (s32[]{:T(128)}, bf16[4,512,1,128]{3,1,2,0:T(8,128)(2,1)}, s32[4]{0:T(128)S(1)}, s32[2048]{0:T(1024)S(1)}, bf16[2048,1,128]{2,0,1:T(8,128)(2,1)S(1)}...) while((s32[]{:T(128)}, ...), condition=%wide.region_4.5_spmd.clone, body=%wide.region_1.4_spmd.clone.sunk | while | flops 548470272 | bytes 13922475 | solution.py:45
  74.6 0.6 dynamic_slice.202
  77.6 1.3 fusion.112
  78.9 0.7 fusion.113
  79.6 1.5 fusion.114
  81.1 0.6 dynamic_slice.202
  84.1 1.3 fusion.112
  85.3 0.7 fusion.113
  86.1 1.5 fusion.114
  90.6 1.3 fusion.112
  91.8 0.7 fusion.113
  92.5 1.5 fusion.114
  97.0 1.3 fusion.112
  98.3 0.7 fusion.113
  99.0 1.5 fusion.114
  100.6 4.9 %all-to-all-start = ((bf16[16,128,128]{2,1,0:T(8,128)(2,1)}), bf16[16,128,128]{2,1,0:T(8,128)(2,1)S(1)}, u32[]{:S(2)}, u32[]{:S(2)}) async-start(bf16[16,128,128]{2,1,0:T(8,128)(2,1)} %bitcast.3), calls=%async_computation | async-start | bytes 1048576 | tf_op jit(solution)/shard_map/all_to_all | solution.py:136
  105.6 20.1 %all-gather.6.cloned.1.call-done = bf16[2048,2048]{1,0:T(8,128)(2,1)} async-done(((bf16[128,2048]{1,0:T(8,128)(2,1)}), bf16[2048,2048]{1,0:T(8,128)(2,1)}) %all-gather.6.cloned.1.call-update) | async-done | bytes 8388624 | tf_op jit(solution)/shard_map/all_gather | solution.py:128
  125.7 5.8 %convert_reduce_fusion = f32[128,2048]{1,0:T(8,128)S(1)} fusion(bf16[16,128,128]{2,1,0:T(8,128)(2,1)S(1)} %all-to-all-done, bf16[16,128,2048]{2,1,0:T(8,128)(2,1)} %bitcast.163), kind=kOutput, calls=%fused_computation.18 | convolution fusion | flops 1086062592 | bytes 9961472 | tf_op jit(solution)/shard_map/gtd,gdo->gto/dot_general | solution.py:139
  131.7 1.0 fusion.49
  133.1 52.8 %all-gather.8.cloned.1.call-done = bf16[2048,2048]{1,0:T(8,128)(2,1)} async-done(((bf16[128,2048]{1,0:T(8,128)(2,1)}), bf16[2048,2048]{1,0:T(8,128)(2,1)}) %all-gather.8.cloned.1.call-update) | async-done | bytes 8388624 | tf_op jit(solution)/shard_map/all_gather | solution.py:150
  186.0 4.8 %convolution_convert_fusion = bf16[16,64,2048]{2,1,0:T(8,128)(2,1)S(1)} fusion(bf16[16,128,2048]{2,1,0:T(8,128)(2,1)} %bitcast.160, s32[16,128]{1,0:T(8,128)S(1)} %bitcast_subtract_fusion, pred[16,128]{1,0:T(8,128)(4,1)S(1)} %broadcast_compare_fusion.1), kind=kOutput, calls=%fused_computation.32 | convolution fusion | flops 539230208 | bytes 12593152 | tf_op jit(solution)/shard_map/bst,btd->bsd/dot_general | solution.py:179
  190.8 9.6 %fusion.19 = f32[1024,1408]{1,0:T(8,128)S(1)} fusion(bf16[1024,2048]{1,0:T(8,128)(2,1)S(1)} %bitcast.164, bf16[1,2048,1408]{2,1,0:T(8,128)(2,1)} %param.30), kind=kOutput, calls=%fused_computation.27 | convolution fusion | flops 5905580032 | bytes 15728640 | tf_op jit(solution)/shard_map/dot_general | solution.py:183
  200.4 7.0 %multiply_convert_fusion = bf16[1024,1408]{1,0:T(8,128)(2,1)S(1)} fusion(f32[1024,1408]{1,0:T(8,128)S(1)} %fusion.19, bf16[1024,2048]{1,0:T(8,128)(2,1)S(1)} %bitcast.165, bf16[1,2048,1408]{2,1,0:T(8,128)(2,1)S(1)} %bitcast.178), kind=kOutput, calls=%fused_computation.29 | convolution fusion | flops 5914230784 | bytes 18612224 | tf_op jit(solution)/shard_map/dot_general | solution.py:185
  207.5 3.6 %fusion.30 = bf16[1024,1024]{1,0:T(8,128)(2,1)S(1)} fusion(bf16[1024,1408]{1,0:T(8,128)(2,1)S(1)} %multiply_convert_fusion, bf16[1408,2048]{1,0:T(8,128)(2,1)S(1)} %bitcast.181), kind=kOutput, calls=%fused_computation.43 | convolution fusion | flops 2953838592 | bytes 7864320 | tf_op jit(solution)/shard_map/dot_general | solution.py:199
  211.2 3.6 %fusion.27 = bf16[1024,1024]{1,0:T(8,128)(2,1)S(1)} fusion(bf16[1024,1408]{1,0:T(8,128)(2,1)S(1)} %multiply_convert_fusion, bf16[1408,2048]{1,0:T(8,128)(2,1)S(1)} %bitcast.182), kind=kOutput, calls=%fused_computation.42 | convolution fusion | flops 2953838592 | bytes 7864320 | tf_op jit(solution)/shard_map/dot_general | solution.py:199
  214.9 3.2 %fusion.39 = f32[2048,352]{0,1:T(8,128)S(1)} fusion(bf16[2048,2048]{1,0:T(8,128)(2,1)S(1)} %bitcast.162, bf16[2048,176]{0,1:T(8,128)(2,1)S(1)} %copy-done.9, bf16[2048,176]{0,1:T(8,128)(2,1)S(1)} %copy-done.10), kind=kOutput, calls=%fused_computation.57 | convolution fusion | flops 2955673600 | bytes 12713984 | tf_op jit(solution)/shard_map/dot_general | solution.py:174
  218.5 1.3 convolution_convert_fusion.2
  219.8 11.6 %fusion.14 = bf16[2048,1024]{1,0:T(8,128)(2,1)S(1)} fusion(bf16[2048,1024]{1,0:T(8,128)(2,1)S(1)} %bitcast.167, bf16[2048,176]{0,1:T(8,128)(2,1)S(1)} %fusion.38, f32[2048]{0:T(1024)S(1)} %get-tuple-element.82, bf16[176,2048]{1,0:T(8,128)(2,1)S(1)} %copy-done.11), kind=kOutput, calls=%fused_computation.21 | convolution fusion | flops 746586112 | bytes 9478144 | tf_op jit(solution)/shard_map/dot_general | solution.py:197
  231.5 1.8 dynamic-slice_bitcast_fusion
  233.5 1.3 convolution_convert_fusion.3
  234.8 1.7 fusion.16
  236.5 2.0 copy-done.1
  239.1 3.2 %convert_add_fusion = f32[4,2,128,1024]{3,2,1,0:T(8,128)S(1)} fusion(bf16[4,2,128,1024]{3,2,1,0:T(8,128)(2,1)} %collective-permute-done.8, bf16[4,2,2,128,1024]{4,3,2,1,0:T(8,128)(2,1)} %bitcast.171, s32[]{:T(128)S(6)} %select_n.134), kind=kLoop, calls=%fused_computation.30 | loop fusion | flops 3145728 | bytes 8388612 | tf_op jit(solution)/shard_map/add | solution.py:69
  242.2 0.6 fusion.92
  242.9 1.6 collective-permute-start.9
  244.5 1.8 collective-permute-start.12
  246.3 2.5 convert_add_fusion.1
  248.8 0.6 fusion.91
  249.9 3.0 collective-permute-start.4
  253.0 0.8 collective-permute-start.10
  253.8 2.6 collective-permute-start.13
  256.4 3.7 %collective-permute-done.1 = bf16[2,128,512]{2,1,0:T(8,128)(2,1)S(1)} collective-permute-done((bf16[2,128,512]{2,1,0:T(8,128)(2,1)S(1)}, bf16[2,128,512]{2,1,0:T(8,128)(2,1)S(1)}, u32[]{:S(2)}, u32[]{:S(2)}) %collective-permute-start.1) | collective-permute-done | bytes 262176 | tf_op jit(solution)/shard_map/ppermute | solution.py:80
  260.3 3.3 %collective-permute-start.5 = (bf16[2,128,512]{2,1,0:T(8,128)(2,1)S(1)}, bf16[2,128,512]{2,1,0:T(8,128)(2,1)S(1)}, u32[]{:S(2)}, u32[]{:S(2)}) collective-permute-start(bf16[2,128,512]{2,1,0:T(8,128)(2,1)S(1)} %fusion.66), channel_id=1, source_target_pairs={{0,12},{1,13},{2,14},{3,15},{4,0},{5,1},{6,2},{7,3},{8,4},{9,5},{1... | collective-permute-start | bytes 786440 | tf_op jit(solution)/shard_map/ppermute | solution.py:81
  263.6 2.1 collective-permute-done.10
  265.9 3.3 %collective-permute-start.14 = (bf16[2,128,512]{2,1,0:T(8,128)(2,1)S(1)}, bf16[2,128,512]{2,1,0:T(8,128)(2,1)S(1)}, u32[]{:S(2)}, u32[]{:S(2)}) collective-permute-start(bf16[2,128,512]{2,1,0:T(8,128)(2,1)S(1)} %fusion.61), channel_id=1, source_target_pairs={{0,12},{1,13},{2,14},{3,15},{4,0},{5,1},{6,2},{7,3},{8,4},{9,5},{1... | collective-permute-start | bytes 786440 | tf_op jit(solution)/shard_map/ppermute | solution.py:81
  269.2 2.1 collective-permute-done.2
  271.6 3.3 %collective-permute-start.6 = (bf16[2,128,512]{2,1,0:T(8,128)(2,1)S(1)}, bf16[2,128,512]{2,1,0:T(8,128)(2,1)S(1)}, u32[]{:S(2)}, u32[]{:S(2)}) collective-permute-start(bf16[2,128,512]{2,1,0:T(8,128)(2,1)S(1)} %fusion.65), channel_id=1, source_target_pairs={{0,12},{1,13},{2,14},{3,15},{4,0},{5,1},{6,2},{7,3},{8,4},{9,5},{1... | collective-permute-start | bytes 786440 | tf_op jit(solution)/shard_map/ppermute | solution.py:81
  274.8 2.1 collective-permute-done.11
  277.1 1.5 collective-permute-start.15
  278.6 2.6 collective-permute-done.3
  281.4 0.7 fusion.79
  282.1 1.4 collective-permute-start.7
  283.5 1.1 maximum_bitcast_fusion
  284.6 1.2 broadcast_in_dim.27
  285.8 3.4 %scatter_fusion = bf16[2,16,128,128]{3,2,1,0:T(8,128)(2,1)} fusion(bf16[2,16,128,128]{3,2,1,0:T(8,128)(2,1)} %broadcast_in_dim.27, s32[16]{0:T(128)S(1)} %compare_select_fusion, bf16[16,2,128,128]{3,2,1,0:T(8,128)(2,1)} %maximum_bitcast_fusion), kind=kCustom, calls=%fused_computation | custom fusion | bytes 3145792 | tf_op jit(solution)/shard_map/scatter | solution.py:134
  289.2 1.0 fusion.55
  290.2 1.0 fusion.60
  291.2 0.9 fusion.50
  (103 shorter events, 7.5 us)
Async XLA Ops:
  7.2 58.1 %all-gather.4.cloned.1.call-start = ((), (), s32[]{:S(2)}) async-start(), calls=%async_computation.1 | async-start | bytes 8912896 | tf_op jit(solution)/shard_map/all_gather | solution.py:127
  10.5 115.1 %all-gather.6.cloned.1.call-start = ((), (), s32[]{:S(2)}) async-start(), calls=%async_computation.2 | async-start | bytes 8912896 | tf_op jit(solution)/shard_map/all_gather | solution.py:128
  73.5 1.2 copy-start.7
  100.6 25.1 %all-to-all-start = ((bf16[16,128,128]{2,1,0:T(8,128)(2,1)}), bf16[16,128,128]{2,1,0:T(8,128)(2,1)S(1)}, u32[]{:S(2)}, u32[]{:S(2)}) async-start(bf16[16,128,128]{2,1,0:T(8,128)(2,1)} %bitcast.3), calls=%async_computation | async-start | bytes 1048576 | tf_op jit(solution)/shard_map/all_to_all | solution.py:136
  105.5 80.5 %all-gather.8.cloned.1.call-start = ((), (), s32[]{:S(2)}) async-start(), calls=%async_computation.3 | async-start | bytes 8912896 | tf_op jit(solution)/shard_map/all_gather | solution.py:150
  125.6 5.8 %copy-start = (bf16[128,2048]{1,0:T(8,128)(2,1)S(1)}, bf16[128,2048]{1,0:T(8,128)(2,1)}, u32[]{:S(2)}) copy-start(bf16[128,2048]{1,0:T(8,128)(2,1)} %param.19) | copy-start | bytes 1572868
  125.6 6.1 %copy-start.8 = (f32[2048]{0:T(1024)S(1)}, f32[2048]{0:T(1024)}, u32[]{:S(2)}) copy-start(f32[2048]{0:T(1024)} %param.26) | copy-start | bytes 24580
  125.6 7.1 %copy-start.5 = (f32[2048,6]{0,1:T(8,128)S(1)}, f32[2048,6]{0,1:T(8,128)}, u32[]{:S(2)}) copy-start(f32[2048,6]{0,1:T(8,128)} %param.34) | copy-start | bytes 147460
  125.6 7.1 %copy-start.6 = (s32[2048,6]{0,1:T(8,128)S(1)}, s32[2048,6]{0,1:T(8,128)}, u32[]{:S(2)}) copy-start(s32[2048,6]{0,1:T(8,128)} %param.33) | copy-start | bytes 147460
  186.0 14.4 %slice-start.2 = ((s8[5767168]{0:T(1024)(128)(4,1)}), s8[4194304]{0:T(1024)(128)(4,1)S(1)}, s32[]{:S(2)}) async-start(s8[5767168]{0:T(1024)(128)(4,1)} %bitcast.177), calls=%async_computation.6 | async-start | bytes 8388608
  190.8 9.7 %slice-start.3 = ((s8[5767168]{0:T(1024)(128)(4,1)}), s8[1572864]{0:T(1024)(128)(4,1)S(1)}, s32[]{:S(2)}) async-start(s8[5767168]{0:T(1024)(128)(4,1)} %bitcast.177), calls=%async_computation.7 | async-start | bytes 3145728
  190.8 16.7 %slice-start.4 = ((s8[5767168]{0:T(1024)(128)(4,1)}), s8[4194304]{0:T(1024)(128)(4,1)S(1)}, s32[]{:S(2)}) async-start(s8[5767168]{0:T(1024)(128)(4,1)} %bitcast.179), calls=%async_computation.8 | async-start | bytes 8388608
  200.4 7.1 %slice-start.5 = ((s8[5767168]{0:T(1024)(128)(4,1)}), s8[1572864]{0:T(1024)(128)(4,1)S(1)}, s32[]{:S(2)}) async-start(s8[5767168]{0:T(1024)(128)(4,1)} %bitcast.179), calls=%async_computation.9 | async-start | bytes 3145728
  207.5 7.3 %slice-start = ((s8[8388608]{0:T(1024)(128)(4,1)}), s8[4194304]{0:T(1024)(128)(4,1)S(1)}, s32[]{:S(2)}) async-start(s8[8388608]{0:T(1024)(128)(4,1)} %bitcast.161), calls=%async_computation.4 | async-start | bytes 8388608
  211.2 3.7 %slice-start.1 = ((s8[8388608]{0:T(1024)(128)(4,1)}), s8[4194304]{0:T(1024)(128)(4,1)S(1)}, s32[]{:S(2)}) async-start(s8[8388608]{0:T(1024)(128)(4,1)} %bitcast.161), calls=%async_computation.5 | async-start | bytes 8388608
  211.2 3.7 %copy-start.9 = (bf16[2048,176]{0,1:T(8,128)(2,1)S(1)}, bf16[2048,176]{0,1:T(8,128)(2,1)}, u32[]{:S(2)}) copy-start(bf16[2048,176]{0,1:T(8,128)(2,1)} %param.28) | copy-start | bytes 2162692
  211.2 3.7 %copy-start.10 = (bf16[2048,176]{0,1:T(8,128)(2,1)S(1)}, bf16[2048,176]{0,1:T(8,128)(2,1)}, u32[]{:S(2)}) copy-start(bf16[2048,176]{0,1:T(8,128)(2,1)} %param.27) | copy-start | bytes 2162692
  218.1 1.7 copy-start.11
  231.5 3.3 %copy-start.3 = (bf16[2048,1024]{1,0:T(8,128)(2,1)}, bf16[2048,1024]{1,0:T(8,128)(2,1)S(1)}, u32[]{:S(2)}) copy-start(bf16[2048,1024]{1,0:T(8,128)(2,1)S(1)} %fusion.14) | copy-start | bytes 12582916
  233.3 5.8 %collective-permute-start.8 = (bf16[4,2,128,1024]{3,2,1,0:T(8,128)(2,1)}, bf16[4,2,128,1024]{3,2,1,0:T(8,128)(2,1)}, u32[]{:S(2)}, u32[]{:S(2)}) collective-permute-start(bf16[4,2,128,1024]{3,2,1,0:T(8,128)(2,1)} %dynamic-slice_bitcast_fusion), channel_id=1, source_target_pairs={{0,1},{1,0},{2,3},{3,2},{4,5},{5,4},{6,7},{7,6},{8,9},{9,8},{10,11... | collective-permute-start | bytes 6291464 | tf_op jit(solution)/shard_map/ppermute | solution.py:68
  236.5 2.0 copy-start.1
  236.5 2.5 copy-start.12
  238.7 7.6 %collective-permute-start = (bf16[4,2,128,1024]{3,2,1,0:T(8,128)(2,1)S(1)}, bf16[4,2,128,1024]{3,2,1,0:T(8,128)(2,1)}, u32[]{:S(2)}, u32[]{:S(2)}) collective-permute-start(bf16[4,2,128,1024]{3,2,1,0:T(8,128)(2,1)S(1)} %dynamic-slice_bitcast_fusion.1), channel_id=1, source_target_pairs={{0,1},{1,0},{2,3},{3,2},{4,5},{5,4},{6,7},{7,6},{8,9},{9,8},{10,11... | collective-permute-start | bytes 6291464 | tf_op jit(solution)/shard_map/ppermute | solution.py:68
  242.2 4.1 %copy-start.2 = (bf16[2048,1024]{1,0:T(8,128)(2,1)S(1)}, bf16[2048,1024]{1,0:T(8,128)(2,1)}, u32[]{:S(2)}) copy-start(bf16[2048,1024]{1,0:T(8,128)(2,1)} %copy-done.1) | copy-start | bytes 12582916
  242.9 10.0 %collective-permute-start.9 = (bf16[2,128,512]{2,1,0:T(8,128)(2,1)S(1)}, bf16[2,128,512]{2,1,0:T(8,128)(2,1)S(1)}, u32[]{:S(2)}, u32[]{:S(2)}) collective-permute-start(bf16[2,128,512]{2,1,0:T(8,128)(2,1)S(1)} %fusion.77), channel_id=1, source_target_pairs={{0,4},{1,5},{2,6},{3,7},{4,8},{5,9},{6,10},{7,11},{8,12},{9,13},{1... | collective-permute-start | bytes 786440 | tf_op jit(solution)/shard_map/ppermute | solution.py:80
  244.5 9.2 %collective-permute-start.12 = (bf16[2,128,512]{2,1,0:T(8,128)(2,1)S(1)}, bf16[2,128,512]{2,1,0:T(8,128)(2,1)S(1)}, u32[]{:S(2)}, u32[]{:S(2)}) collective-permute-start(bf16[2,128,512]{2,1,0:T(8,128)(2,1)S(1)} %fusion.78), channel_id=1, source_target_pairs={{0,12},{1,13},{2,14},{3,15},{4,0},{5,1},{6,2},{7,3},{8,4},{9,5},{1... | collective-permute-start | bytes 786440 | tf_op jit(solution)/shard_map/ppermute | solution.py:81
  249.6 10.5 %collective-permute-start.1 = (bf16[2,128,512]{2,1,0:T(8,128)(2,1)S(1)}, bf16[2,128,512]{2,1,0:T(8,128)(2,1)S(1)}, u32[]{:S(2)}, u32[]{:S(2)}) collective-permute-start(bf16[2,128,512]{2,1,0:T(8,128)(2,1)S(1)} %fusion.75), channel_id=1, source_target_pairs={{0,4},{1,5},{2,6},{3,7},{4,8},{5,9},{6,10},{7,11},{8,12},{9,13},{1... | collective-permute-start | bytes 786440 | tf_op jit(solution)/shard_map/ppermute | solution.py:80
  249.9 10.3 %collective-permute-start.4 = (bf16[2,128,512]{2,1,0:T(8,128)(2,1)S(1)}, bf16[2,128,512]{2,1,0:T(8,128)(2,1)S(1)}, u32[]{:S(2)}, u32[]{:S(2)}) collective-permute-start(bf16[2,128,512]{2,1,0:T(8,128)(2,1)S(1)} %fusion.76), channel_id=1, source_target_pairs={{0,12},{1,13},{2,14},{3,15},{4,0},{5,1},{6,2},{7,3},{8,4},{9,5},{1... | collective-permute-start | bytes 786440 | tf_op jit(solution)/shard_map/ppermute | solution.py:81
  253.0 12.7 %collective-permute-start.10 = (bf16[2,128,512]{2,1,0:T(8,128)(2,1)S(1)}, bf16[2,128,512]{2,1,0:T(8,128)(2,1)S(1)}, u32[]{:S(2)}, u32[]{:S(2)}) collective-permute-start(bf16[2,128,512]{2,1,0:T(8,128)(2,1)S(1)} %fusion.64), channel_id=1, source_target_pairs={{0,4},{1,5},{2,6},{3,7},{4,8},{5,9},{6,10},{7,11},{8,12},{9,13},{1... | collective-permute-start | bytes 786440 | tf_op jit(solution)/shard_map/ppermute | solution.py:80
  253.8 12.0 %collective-permute-start.13 = (bf16[2,128,512]{2,1,0:T(8,128)(2,1)S(1)}, bf16[2,128,512]{2,1,0:T(8,128)(2,1)S(1)}, u32[]{:S(2)}, u32[]{:S(2)}) collective-permute-start(bf16[2,128,512]{2,1,0:T(8,128)(2,1)S(1)} %fusion.62), channel_id=1, source_target_pairs={{0,12},{1,13},{2,14},{3,15},{4,0},{5,1},{6,2},{7,3},{8,4},{9,5},{1... | collective-permute-start | bytes 786440 | tf_op jit(solution)/shard_map/ppermute | solution.py:81
  260.1 11.2 %collective-permute-start.2 = (bf16[2,128,512]{2,1,0:T(8,128)(2,1)S(1)}, bf16[2,128,512]{2,1,0:T(8,128)(2,1)S(1)}, u32[]{:S(2)}, u32[]{:S(2)}) collective-permute-start(bf16[2,128,512]{2,1,0:T(8,128)(2,1)S(1)} %fusion.68), channel_id=1, source_target_pairs={{0,4},{1,5},{2,6},{3,7},{4,8},{5,9},{6,10},{7,11},{8,12},{9,13},{1... | collective-permute-start | bytes 786440 | tf_op jit(solution)/shard_map/ppermute | solution.py:80
  260.3 11.1 %collective-permute-start.5 = (bf16[2,128,512]{2,1,0:T(8,128)(2,1)S(1)}, bf16[2,128,512]{2,1,0:T(8,128)(2,1)S(1)}, u32[]{:S(2)}, u32[]{:S(2)}) collective-permute-start(bf16[2,128,512]{2,1,0:T(8,128)(2,1)S(1)} %fusion.66), channel_id=1, source_target_pairs={{0,12},{1,13},{2,14},{3,15},{4,0},{5,1},{6,2},{7,3},{8,4},{9,5},{1... | collective-permute-start | bytes 786440 | tf_op jit(solution)/shard_map/ppermute | solution.py:81
  265.8 11.2 %collective-permute-start.11 = (bf16[2,128,512]{2,1,0:T(8,128)(2,1)S(1)}, bf16[2,128,512]{2,1,0:T(8,128)(2,1)S(1)}, u32[]{:S(2)}, u32[]{:S(2)}) collective-permute-start(bf16[2,128,512]{2,1,0:T(8,128)(2,1)S(1)} %fusion.63), channel_id=1, source_target_pairs={{0,4},{1,5},{2,6},{3,7},{4,8},{5,9},{6,10},{7,11},{8,12},{9,13},{1... | collective-permute-start | bytes 786440 | tf_op jit(solution)/shard_map/ppermute | solution.py:80
  265.9 11.1 %collective-permute-start.14 = (bf16[2,128,512]{2,1,0:T(8,128)(2,1)S(1)}, bf16[2,128,512]{2,1,0:T(8,128)(2,1)S(1)}, u32[]{:S(2)}, u32[]{:S(2)}) collective-permute-start(bf16[2,128,512]{2,1,0:T(8,128)(2,1)S(1)} %fusion.61), channel_id=1, source_target_pairs={{0,12},{1,13},{2,14},{3,15},{4,0},{5,1},{6,2},{7,3},{8,4},{9,5},{1... | collective-permute-start | bytes 786440 | tf_op jit(solution)/shard_map/ppermute | solution.py:81
  271.4 9.8 %collective-permute-start.3 = (bf16[2,128,512]{2,1,0:T(8,128)(2,1)S(1)}, bf16[2,128,512]{2,1,0:T(8,128)(2,1)S(1)}, u32[]{:S(2)}, u32[]{:S(2)}) collective-permute-start(bf16[2,128,512]{2,1,0:T(8,128)(2,1)S(1)} %fusion.67), channel_id=1, source_target_pairs={{0,4},{1,5},{2,6},{3,7},{4,8},{5,9},{6,10},{7,11},{8,12},{9,13},{1... | collective-permute-start | bytes 786440 | tf_op jit(solution)/shard_map/ppermute | solution.py:80
  271.6 12.0 %copy-start.4 = (bf16[2048,128]{1,0:T(8,128)(2,1)S(1)}, bf16[2048,128]{1,0:T(8,128)(2,1)}, u32[]{:S(2)}) copy-start(bf16[2048,128]{1,0:T(8,128)(2,1)} %get-tuple-element.95) | copy-start | bytes 1572868
  271.6 9.7 %collective-permute-start.6 = (bf16[2,128,512]{2,1,0:T(8,128)(2,1)S(1)}, bf16[2,128,512]{2,1,0:T(8,128)(2,1)S(1)}, u32[]{:S(2)}, u32[]{:S(2)}) collective-permute-start(bf16[2,128,512]{2,1,0:T(8,128)(2,1)S(1)} %fusion.65), channel_id=1, source_target_pairs={{0,12},{1,13},{2,14},{3,15},{4,0},{5,1},{6,2},{7,3},{8,4},{9,5},{1... | collective-permute-start | bytes 786440 | tf_op jit(solution)/shard_map/ppermute | solution.py:81
  277.1 12.1 %collective-permute-start.15 = (bf16[128,1024]{1,0:T(8,128)(2,1)S(1)}, bf16[128,1024]{1,0:T(8,128)(2,1)}, u32[]{:S(2)}, u32[]{:S(2)}) collective-permute-start(bf16[128,1024]{1,0:T(8,128)(2,1)S(1)} %fusion.80), channel_id=1, source_target_pairs={{0,2},{1,3},{2,0},{3,1},{4,6},{5,7},{6,4},{7,5},{8,10},{9,11},{10,... | collective-permute-start | bytes 786440 | tf_op jit(solution)/shard_map/ppermute | solution.py:96
  282.1 8.1 %collective-permute-start.7 = (bf16[128,1024]{1,0:T(8,128)(2,1)}, bf16[128,1024]{1,0:T(8,128)(2,1)}, u32[]{:S(2)}, u32[]{:S(2)}) collective-permute-start(bf16[128,1024]{1,0:T(8,128)(2,1)} %fusion.79), channel_id=1, source_target_pairs={{0,2},{1,3},{2,0},{3,1},{4,6},{5,7},{6,4},{7,5},{8,10},{9,11},{10,... | collective-permute-start | bytes 786440 | tf_op jit(solution)/shard_map/ppermute | solution.py:96
Sparse Core Ops, SparseCore 0:
  10.6 54.5 all-gather.3
  66.9 58.6 all-gather.5
  132.9 53.0 all-gather.7

commit v5 on v4

--- a/solution.py
+++ b/solution.py
@@ -97,6 +97,34 @@
     return keep_side + got_side.astype(jnp.float32)
 
 
+def weight_gather(block, groups):
+    ring = groups // 4
+    me = lax.axis_index("tensor")
+    y = me // 4
+    side = (me // 2) % 2
+    core = me % 2
+    side_pairs = [(t, t ^ 2) for t in range(groups)]
+    core_pairs = [(t, t ^ 1) for t in range(groups)]
+    forward_pairs = [(t, ((t // 4 + 1) % ring) * 4 + t % 4) for t in range(groups)]
+    backward_pairs = [(t, ((t // 4 + ring - 1) % ring) * 4 + t % 4) for t in range(groups)]
+    other_side = lax.ppermute(block, "tensor", side_pairs)
+    pair = jnp.stack([block, other_side])
+    from_prev = lax.ppermute(pair, "tensor", forward_pairs)
+    from_next = lax.ppermute(pair, "tensor", backward_pairs)
+    half = block.shape[1] // 2
+    far_a = lax.ppermute(from_prev[..., :half], "tensor", forward_pairs)
+    far_b = lax.ppermute(from_next[..., half:], "tensor", backward_pairs)
+    far = jnp.concatenate([far_a, far_b], axis=-1)
+    mine = jnp.stack([pair, from_next, far, from_prev])
+    other_core = lax.ppermute(mine, "tensor", core_pairs)
+    offsets = jnp.array([0, 1, 2, ring - 1], jnp.int32)
+    rows_y = (y + offsets) % ring
+    sides = jnp.stack([side, 1 - side])
+    owner_mine = (rows_y[:, None] * 2 + sides[None, :]) * 2 + core
+    owner_other = owner_mine - core + (1 - core)
+    return (mine, other_core), (owner_mine, owner_other)
+
+
 def shards(
     tokens,
     segment_ids,
@@ -125,7 +153,7 @@
 
     projection = jnp.concatenate([query_weight, key_weight, value_weight], axis=1)
     normed_all = lax.all_gather(rms_scale(tokens, attention_gain), "tensor", axis=0, tiled=True)
-    out_weight_all = lax.all_gather(output_weight, "tensor", axis=0, tiled=True)
+    weight_pieces, piece_owners = weight_gather(output_weight, groups)
     projected = jnp.dot(normed_all, projection, preferred_element_type=jnp.float32).astype(
         jnp.bfloat16
     )
@@ -136,13 +164,16 @@
     received = lax.all_to_all(
         context.reshape(groups, tok_dev, inner), "tensor", split_axis=0, concat_axis=0, tiled=True
     )
-    partials = jnp.einsum(
-        "gtd,gdo->gto",
-        received,
-        out_weight_all.reshape(groups, inner, model_width),
-        preferred_element_type=jnp.float32,
-    ).astype(jnp.bfloat16)
-    attention = jnp.sum(partials.astype(jnp.float32), axis=0)
+    attention = jnp.zeros((tok_dev, model_width), jnp.float32)
+    for weight_piece, owner in zip(weight_pieces, piece_owners):
+        context_piece = jnp.take(received, owner.reshape(-1), axis=0)
+        partials = jnp.einsum(
+            "gtd,gdo->gto",
+            context_piece,
+            weight_piece.reshape(-1, inner, model_width),
+            preferred_element_type=jnp.float32,
+        ).astype(jnp.bfloat16)
+        attention = attention + jnp.sum(partials.astype(jnp.float32), axis=0)
     residual = (tokens.astype(jnp.float32) + attention).astype(jnp.bfloat16)
     normed_ffn = rms_scale(residual, ffn_gain)
     pieces = 2

time: 303 us -> 332 us (1.096)
  waiting for transfers between devices: 140 us -> 149 us
  starting transfers between devices: 28.6 us -> 35.9 us
  other arithmetic: 21.7 us -> 28 us
    ppermute x0 -> x6, waiting for transfers between devices: none -> 75.6 us  [the longest x1 44.3 us: weight_gather(): from_next = lax.ppermute(pair, 'tensor', backward_pairs)]
    all_gather x1, waiting for transfers between devices: 53.9 us -> 0.01 us  [shards(): lax.all_gather(rms_scale(tokens, attention_gain), 'tensor', axis=0, tiled...]
    all_gather x1 -> x0, waiting for transfers between devices: 20.1 us -> none  [shards(): out_weight_all = lax.all_gather(output_weight, 'tensor', axis=0, tiled=True)]
    all_to_all x1, waiting for transfers between devices: 0.01 us -> 10.5 us  [shards(): lax.all_to_all(context.reshape(groups, tok_dev, inner), 'tensor', split_a...]
    ppermute x0 -> x6, starting transfers between devices: none -> 6.95 us  [the longest x1 3.03 us: weight_gather(): from_next = lax.ppermute(pair, 'tensor', backward_pairs)]
    another operation x0 -> x4, other arithmetic: none -> 5.81 us  [the longest x3 5.73 us: weight_gather(): mine = jnp.stack([pair, from_next, far, from_prev])]
    dot_general x1 -> x2, matrix products: 5.81 us -> 7.13 us  [shards(): jnp.einsum('gtd,gdo->gto', context_piece, weight_piece.reshape(-1, inner,...]
  transfers between devices with their start and end apart: 20 -> 25, of which waited for: 8 -> 10; matrix products, arithmetic and copies ran while one was open for 16% -> 18% of each run, Pallas kernels for 0% -> 0%
where the time goes in v5:
time: 332 us; the launch traced here: 327 us
  waiting for transfers between devices  149 us (45%)
  matrix products  74.2 us (22%)
  starting transfers between devices  35.9 us (11%)
  other arithmetic  28 us (8%)
  local copies, waits for them, and re-layouts  16.9 us (5%)
  between operations  15 us (5%)
  loops' own time  7.82 us (2%)
    all_gather x1, waiting for transfers between devices, shards(): normed_stream = lax.all_gather(normed_ffn, 'tensor', axis=0, tiled=True)  50.7 us
    ppermute x1, waiting for transfers between devices, weight_gather(): from_next = lax.ppermute(pair, 'tensor', backward_pairs)  44.3 us
    ppermute x1, waiting for transfers between devices, weight_gather(): far_b = lax.ppermute(from_next[..., half:], 'tensor', backward_pairs)  17.2 us
    ppermute x6, starting transfers between devices, ring_reduce_scatter(): recv_b = lax.ppermute(carry_b, 'tensor', backward_pairs)  17.2 us
    ppermute x1, waiting for transfers between devices, weight_gather(): other_side = lax.ppermute(block, 'tensor', side_pairs)  14.1 us
    dot_general x2, matrix products, shards(): jnp.dot(hidden_all, shared_down[:, columns], preferred_element_type=jnp.f...  13.3 us
    ppermute x6, waiting for transfers between devices, ring_reduce_scatter(): recv_f = lax.ppermute(carry_f, 'tensor', forward_pairs)  12.5 us
    all_to_all x1, waiting for transfers between devices, shards(): lax.all_to_all(context.reshape(groups, tok_dev, inner), 'tensor', split_a...  10.5 us
  transfers between devices with their start and end apart: 25, of which 10 were waited for; matrix products, arithmetic and copies ran while one was open for 18% of the time, Pallas kernels for 0%

profile of v5, /device:TPU:0, one launch (start us, length us, event | category | flops | bytes accessed | tf_op | source)
XLA Modules:
  0.0 327.2 jit_solution(1934711890195414165)
XLA Ops:
  7.2 1.2 fusion.43
  8.4 2.0 fusion.45
  10.5 1.7 collective-permute-start
  12.2 14.1 %collective-permute-done = bf16[128,2048]{1,0:T(8,128)(2,1)S(1)} collective-permute-done((bf16[128,2048]{1,0:T(8,128)(2,1)}, bf16[128,2048]{1,0:T(8,128)(2,1)S(1)}, u32[]{:S(2)}, u32[]{:S(2)}) %collective-permute-start) | collective-permute-done | bytes 524320 | tf_op jit(solution)/shard_map/ppermute | solution.py:110
  26.2 2.2 fusion.101
  28.4 3.0 collective-permute-start.1
  31.5 44.3 %collective-permute-done.1 = bf16[2,128,2048]{2,1,0:T(8,128)(2,1)S(1)} collective-permute-done((bf16[2,128,2048]{2,1,0:T(8,128)(2,1)}, bf16[2,128,2048]{2,1,0:T(8,128)(2,1)S(1)}, u32[]{:S(2)}, u32[]{:S(2)}) %collective-permute-start.1) | collective-permute-done | bytes 1048608 | tf_op jit(solution)/shard_map/ppermute | solution.py:113
  76.6 0.9 collective-permute-start.4
  77.6 0.8 slice.67
  78.4 1.3 collective-permute-start.3
  80.1 17.2 %collective-permute-done.4 = bf16[2,128,1024]{2,1,0:T(8,128)(2,1)} collective-permute-done((bf16[2,128,1024]{2,1,0:T(8,128)(2,1)}, bf16[2,128,1024]{2,1,0:T(8,128)(2,1)}, u32[]{:S(2)}, u32[]{:S(2)}) %collective-permute-start.4) | collective-permute-done | bytes 524320 | tf_op jit(solution)/shard_map/ppermute | solution.py:116
  97.3 1.3 maximum_bitcast_fusion
  98.6 2.3 pad_maximum_fusion
  100.9 8.3 %convolution_convert_fusion.1 = bf16[2048,384]{1,0:T(8,128)(2,1)S(1)} fusion(bf16[2048,2048]{1,0:T(8,128)(2,1)} %all-gather.3.cloned.1.call-done, bf16[2048,128]{1,0:T(8,128)(2,1)} %param.27, bf16[2048,128]{1,0:T(8,128)(2,1)} %param.26, bf16[2048,128]{1,0:T(8,128)(2,1)} %param.25), kind=kOutput, calls=%fused_computation.41 | convolution fusion | flops 3226730496 | bytes 11534336 | tf_op jit(solution)/shard_map/dot_general | solution.py:157
  109.1 1.2 fusion.106
  110.3 27.1 %while.11 = (s32[]{:T(128)}, bf16[4,512,1,128]{3,1,2,0:T(8,128)(2,1)}, s32[4]{0:T(128)S(1)}, s32[2048]{0:T(1024)S(1)}, bf16[2048,1,128]{2,0,1:T(8,128)(2,1)S(1)}...) while((s32[]{:T(128)}, ...), condition=%wide.region_4.5_spmd.clone, body=%wide.region_1.4_spmd.clone.sunk | while | flops 548470272 | bytes 13922475 | solution.py:45
  113.6 1.3 fusion.125
  115.5 1.5 fusion.127
  120.3 1.3 fusion.125
  122.3 1.5 fusion.127
  127.1 1.3 fusion.125
  129.1 1.5 fusion.127
  133.9 1.3 fusion.125
  135.9 1.5 fusion.127
  137.4 5.1 %all-to-all-start = ((bf16[16,128,128]{2,1,0:T(8,128)(2,1)}), bf16[16,128,128]{2,1,0:T(8,128)(2,1)S(1)}, u32[]{:S(2)}, u32[]{:S(2)}) async-start(bf16[16,128,128]{2,1,0:T(8,128)(2,1)} %bitcast.5), calls=%async_computation | async-start | bytes 1048576 | tf_op jit(solution)/shard_map/all_to_all | solution.py:164
  142.9 10.5 %all-to-all-done = bf16[16,128,128]{2,1,0:T(8,128)(2,1)S(1)} async-done(((bf16[16,128,128]{2,1,0:T(8,128)(2,1)}), bf16[16,128,128]{2,1,0:T(8,128)(2,1)S(1)}, u32[]{:S(2)}, u32[]{:S(2)}) %all-to-all-start) | async-done | bytes 524320 | tf_op jit(solution)/shard_map/all_to_all | solution.py:164
  154.6 3.5 %convert_reduce_fusion.1 = f32[128,2048]{1,0:T(8,128)S(1)} fusion(bf16[8,128,2048]{2,1,0:T(8,128)(2,1)} %bitcast.12, bf16[8,128,128]{2,1,0:T(8,128)(2,1)S(1)} %gather_fusion, pred[8]{0:T(512)(128)(4,1)S(1)} %get-tuple-element.105), kind=kOutput, calls=%fused_computation.27 | convolution fusion | flops 543031296 | bytes 5505032 | tf_op jit(solution)/shard_map/gtd,gdo->gto/dot_general | solution.py:170
  158.2 3.6 %convert_reduce_fusion = f32[128,2048]{1,0:T(8,128)S(1)} fusion(bf16[8,128,2048]{2,1,0:T(8,128)(2,1)} %bitcast.13, bf16[8,128,128]{2,1,0:T(8,128)(2,1)S(1)} %gather_fusion.1, pred[8]{0:T(512)(128)(4,1)S(1)} %get-tuple-element.104), kind=kOutput, calls=%fused_computation.26 | convolution fusion | flops 543031296 | bytes 5505032 | tf_op jit(solution)/shard_map/gtd,gdo->gto/dot_general | solution.py:170
  162.2 1.0 fusion.49
  163.6 50.7 %all-gather.5.cloned.1.call-done = bf16[2048,2048]{1,0:T(8,128)(2,1)} async-done(((bf16[128,2048]{1,0:T(8,128)(2,1)}), bf16[2048,2048]{1,0:T(8,128)(2,1)}) %all-gather.5.cloned.1.call-update) | async-done | bytes 8388624 | tf_op jit(solution)/shard_map/all_gather | solution.py:181
  214.2 4.8 %convolution_convert_fusion = bf16[16,64,2048]{2,1,0:T(8,128)(2,1)S(1)} fusion(bf16[16,128,2048]{2,1,0:T(8,128)(2,1)} %bitcast.171, s32[16,128]{1,0:T(8,128)S(1)} %bitcast_subtract_fusion, pred[16,128]{1,0:T(8,128)(4,1)S(1)} %broadcast_compare_fusion.1), kind=kOutput, calls=%fused_computation.36 | convolution fusion | flops 539230208 | bytes 12593152 | tf_op jit(solution)/shard_map/bst,btd->bsd/dot_general | solution.py:210
  219.0 9.4 %fusion.19 = f32[1024,1408]{1,0:T(8,128)S(1)} fusion(bf16[1024,2048]{1,0:T(8,128)(2,1)S(1)} %bitcast.174, bf16[1,2048,1408]{2,1,0:T(8,128)(2,1)} %param.33), kind=kOutput, calls=%fused_computation.30 | convolution fusion | flops 5905580032 | bytes 15728640 | tf_op jit(solution)/shard_map/dot_general | solution.py:214
  228.4 7.0 %multiply_convert_fusion = bf16[1024,1408]{1,0:T(8,128)(2,1)S(1)} fusion(f32[1024,1408]{1,0:T(8,128)S(1)} %fusion.19, bf16[1024,2048]{1,0:T(8,128)(2,1)S(1)} %bitcast.175, bf16[1,2048,1408]{2,1,0:T(8,128)(2,1)S(1)} %bitcast.192), kind=kOutput, calls=%fused_computation.32 | convolution fusion | flops 5914230784 | bytes 18612224 | tf_op jit(solution)/shard_map/dot_general | solution.py:216
  235.5 3.6 %fusion.30 = bf16[1024,1024]{1,0:T(8,128)(2,1)S(1)} fusion(bf16[1024,1408]{1,0:T(8,128)(2,1)S(1)} %multiply_convert_fusion, bf16[1408,2048]{1,0:T(8,128)(2,1)S(1)} %bitcast.195), kind=kOutput, calls=%fused_computation.47 | convolution fusion | flops 2953838592 | bytes 7864320 | tf_op jit(solution)/shard_map/dot_general | solution.py:230
  239.2 3.6 %fusion.27 = bf16[1024,1024]{1,0:T(8,128)(2,1)S(1)} fusion(bf16[1024,1408]{1,0:T(8,128)(2,1)S(1)} %multiply_convert_fusion, bf16[1408,2048]{1,0:T(8,128)(2,1)S(1)} %bitcast.196), kind=kOutput, calls=%fused_computation.46 | convolution fusion | flops 2953838592 | bytes 7864320 | tf_op jit(solution)/shard_map/dot_general | solution.py:230
  242.9 3.2 fusion.39
  246.5 1.3 convolution_convert_fusion.2
  247.8 11.6 %fusion.14 = bf16[2048,1024]{1,0:T(8,128)(2,1)S(1)} fusion(bf16[2048,1024]{1,0:T(8,128)(2,1)S(1)} %bitcast.177, bf16[2048,176]{0,1:T(8,128)(2,1)S(1)} %fusion.38, f32[2048]{0:T(1024)S(1)} %get-tuple-element.83, bf16[176,2048]{1,0:T(8,128)(2,1)S(1)} %copy-done.11), kind=kOutput, calls=%fused_computation.22 | convolution fusion | flops 746586112 | bytes 9478144 | tf_op jit(solution)/shard_map/dot_general | solution.py:228
  259.5 1.8 dynamic-slice_bitcast_fusion
  261.5 1.3 convolution_convert_fusion.3
  262.8 1.7 fusion.16
  264.6 2.0 copy-done.1
  267.1 3.2 convert_add_fusion
  270.9 1.5 collective-permute-start.15
  272.5 1.8 collective-permute-start.18
  274.4 2.5 convert_add_fusion.1
  277.9 3.0 collective-permute-start.10
  281.9 2.6 collective-permute-start.19
  284.4 3.7 %collective-permute-done.7 = bf16[2,128,512]{2,1,0:T(8,128)(2,1)S(1)} collective-permute-done((bf16[2,128,512]{2,1,0:T(8,128)(2,1)S(1)}, bf16[2,128,512]{2,1,0:T(8,128)(2,1)S(1)}, u32[]{:S(2)}, u32[]{:S(2)}) %collective-permute-start.7) | collective-permute-done | bytes 262176 | tf_op jit(solution)/shard_map/ppermute | solution.py:80
  288.3 3.3 %collective-permute-start.11 = (bf16[2,128,512]{2,1,0:T(8,128)(2,1)S(1)}, bf16[2,128,512]{2,1,0:T(8,128)(2,1)S(1)}, u32[]{:S(2)}, u32[]{:S(2)}) collective-permute-start(bf16[2,128,512]{2,1,0:T(8,128)(2,1)S(1)} %fusion.66), channel_id=1, source_target_pairs={{0,12},{1,13},{2,14},{3,15},{4,0},{5,1},{6,2},{7,3},{8,4},{9,5},{1... | collective-permute-start | bytes 786440 | tf_op jit(solution)/shard_map/ppermute | solution.py:81
  291.6 2.1 collective-permute-done.16
  294.0 3.3 %collective-permute-start.20 = (bf16[2,128,512]{2,1,0:T(8,128)(2,1)S(1)}, bf16[2,128,512]{2,1,0:T(8,128)(2,1)S(1)}, u32[]{:S(2)}, u32[]{:S(2)}) collective-permute-start(bf16[2,128,512]{2,1,0:T(8,128)(2,1)S(1)} %fusion.61), channel_id=1, source_target_pairs={{0,12},{1,13},{2,14},{3,15},{4,0},{5,1},{6,2},{7,3},{8,4},{9,5},{1... | collective-permute-start | bytes 786440 | tf_op jit(solution)/shard_map/ppermute | solution.py:81
  297.2 2.1 collective-permute-done.8
  299.6 3.3 %collective-permute-start.12 = (bf16[2,128,512]{2,1,0:T(8,128)(2,1)S(1)}, bf16[2,128,512]{2,1,0:T(8,128)(2,1)S(1)}, u32[]{:S(2)}, u32[]{:S(2)}) collective-permute-start(bf16[2,128,512]{2,1,0:T(8,128)(2,1)S(1)} %fusion.65), channel_id=1, source_target_pairs={{0,12},{1,13},{2,14},{3,15},{4,0},{5,1},{6,2},{7,3},{8,4},{9,5},{1... | collective-permute-start | bytes 786440 | tf_op jit(solution)/shard_map/ppermute | solution.py:81
  302.9 2.1 collective-permute-done.17
  305.2 1.5 collective-permute-start.21
  306.6 2.6 collective-permute-done.9
  310.2 1.4 collective-permute-start.13
  311.5 1.1 maximum_bitcast_fusion.1
  312.6 1.2 broadcast_in_dim.36
  313.8 3.4 %scatter_fusion = bf16[2,16,128,128]{3,2,1,0:T(8,128)(2,1)} fusion(bf16[2,16,128,128]{3,2,1,0:T(8,128)(2,1)} %broadcast_in_dim.36, s32[16]{0:T(128)S(1)} %compare_select_fusion.2, bf16[16,2,128,128]{3,2,1,0:T(8,128)(2,1)} %maximum_bitcast_fusion.1), kind=kCustom, calls=%fused_computation.2 | custom fusion | bytes 3145792 | tf_op jit(solution)/shard_map/scatter | solution.py:162
  317.2 1.0 fusion.55
  318.2 1.0 fusion.60
  319.3 0.9 fusion.50
  (129 shorter events, 17.3 us)
Async XLA Ops:
  7.2 93.7 %all-gather.3.cloned.1.call-start = ((), (), s32[]{:S(2)}) async-start(), calls=%async_computation.1 | async-start | bytes 8912896 | tf_op jit(solution)/shard_map/all_gather | solution.py:155
  10.5 15.7 %collective-permute-start = (bf16[128,2048]{1,0:T(8,128)(2,1)}, bf16[128,2048]{1,0:T(8,128)(2,1)S(1)}, u32[]{:S(2)}, u32[]{:S(2)}) collective-permute-start(bf16[128,2048]{1,0:T(8,128)(2,1)} %param.28), channel_id=1, source_target_pairs={{0,2},{1,3},{2,0},{3,1},{4,6},{5,7},{6,4},{7,5},{8,10},{9,11},{10,... | collective-permute-start | bytes 1572872 | tf_op jit(solution)/shard_map/ppermute | solution.py:110
  28.4 47.4 %collective-permute-start.1 = (bf16[2,128,2048]{2,1,0:T(8,128)(2,1)}, bf16[2,128,2048]{2,1,0:T(8,128)(2,1)S(1)}, u32[]{:S(2)}, u32[]{:S(2)}) collective-permute-start(bf16[2,128,2048]{2,1,0:T(8,128)(2,1)} %get-tuple-element.99), channel_id=1, source_target_pairs={{0,12},{1,13},{2,14},{3,15},{4,0},{5,1},{6,2},{7,3},{8,4},{9,5},{1... | collective-permute-start | bytes 3145736 | tf_op jit(solution)/shard_map/ppermute | solution.py:113
  31.5 46.1 %collective-permute-start.2 = (bf16[2,128,2048]{2,1,0:T(8,128)(2,1)}, bf16[2,128,2048]{2,1,0:T(8,128)(2,1)S(1)}, u32[]{:S(2)}, u32[]{:S(2)}) collective-permute-start(bf16[2,128,2048]{2,1,0:T(8,128)(2,1)} %get-tuple-element.99), channel_id=1, source_target_pairs={{0,4},{1,5},{2,6},{3,7},{4,8},{5,9},{6,10},{7,11},{8,12},{9,13},{1... | collective-permute-start | bytes 3145736 | tf_op jit(solution)/shard_map/ppermute | solution.py:112
  76.6 20.7 %collective-permute-start.4 = (bf16[2,128,1024]{2,1,0:T(8,128)(2,1)}, bf16[2,128,1024]{2,1,0:T(8,128)(2,1)}, u32[]{:S(2)}, u32[]{:S(2)}) collective-permute-start(bf16[2,128,1024]{2,1,0:T(8,128)(2,1)} %slice.68), channel_id=1, source_target_pairs={{0,12},{1,13},{2,14},{3,15},{4,0},{5,1},{6,2},{7,3},{8,4},{9,5},{1... | collective-permute-start | bytes 1572872 | tf_op jit(solution)/shard_map/ppermute | solution.py:116
  78.4 18.9 %collective-permute-start.3 = (bf16[2,128,1024]{2,1,0:T(8,128)(2,1)}, bf16[2,128,1024]{2,1,0:T(8,128)(2,1)}, u32[]{:S(2)}, u32[]{:S(2)}) collective-permute-start(bf16[2,128,1024]{2,1,0:T(8,128)(2,1)} %slice.67), channel_id=1, source_target_pairs={{0,4},{1,5},{2,6},{3,7},{4,8},{5,9},{6,10},{7,11},{8,12},{9,13},{1... | collective-permute-start | bytes 1572872 | tf_op jit(solution)/shard_map/ppermute | solution.py:115
  100.9 57.3 %collective-permute-start.5 = (bf16[4,2,128,2048]{3,2,1,0:T(8,128)(2,1)}, bf16[4,2,128,2048]{3,2,1,0:T(8,128)(2,1)}, u32[]{:S(2)}, u32[]{:S(2)}) collective-permute-start(bf16[4,2,128,2048]{3,2,1,0:T(8,128)(2,1)} %pad_maximum_fusion), channel_id=1, source_target_pairs={{0,1},{1,0},{2,3},{3,2},{4,5},{5,4},{6,7},{7,6},{8,9},{9,8},{10,11... | collective-permute-start | bytes 12582920 | tf_op jit(solution)/shard_map/ppermute | solution.py:119
  109.1 1.2 copy-start.7
  137.4 16.0 %all-to-all-start = ((bf16[16,128,128]{2,1,0:T(8,128)(2,1)}), bf16[16,128,128]{2,1,0:T(8,128)(2,1)S(1)}, u32[]{:S(2)}, u32[]{:S(2)}) async-start(bf16[16,128,128]{2,1,0:T(8,128)(2,1)} %bitcast.5), calls=%async_computation | async-start | bytes 1048576 | tf_op jit(solution)/shard_map/all_to_all | solution.py:164
  142.5 71.7 %all-gather.5.cloned.1.call-start = ((), (), s32[]{:S(2)}) async-start(), calls=%async_computation.2 | async-start | bytes 8912896 | tf_op jit(solution)/shard_map/all_gather | solution.py:181
  158.2 3.6 %copy-start = (bf16[128,2048]{1,0:T(8,128)(2,1)S(1)}, bf16[128,2048]{1,0:T(8,128)(2,1)}, u32[]{:S(2)}) copy-start(bf16[128,2048]{1,0:T(8,128)(2,1)} %param.22) | copy-start | bytes 1572868
  158.2 4.0 %copy-start.8 = (f32[2048]{0:T(1024)S(1)}, f32[2048]{0:T(1024)}, u32[]{:S(2)}) copy-start(f32[2048]{0:T(1024)} %param.29) | copy-start | bytes 24580
  161.8 1.4 copy-start.5
  161.8 1.4 copy-start.6
  214.2 14.2 %slice-start.2 = ((s8[5767168]{0:T(1024)(128)(4,1)}), s8[4194304]{0:T(1024)(128)(4,1)S(1)}, s32[]{:S(2)}) async-start(s8[5767168]{0:T(1024)(128)(4,1)} %bitcast.191), calls=%async_computation.5 | async-start | bytes 8388608
  219.0 9.4 %slice-start.3 = ((s8[5767168]{0:T(1024)(128)(4,1)}), s8[1572864]{0:T(1024)(128)(4,1)S(1)}, s32[]{:S(2)}) async-start(s8[5767168]{0:T(1024)(128)(4,1)} %bitcast.191), calls=%async_computation.6 | async-start | bytes 3145728
  219.0 16.5 %slice-start.4 = ((s8[5767168]{0:T(1024)(128)(4,1)}), s8[4194304]{0:T(1024)(128)(4,1)S(1)}, s32[]{:S(2)}) async-start(s8[5767168]{0:T(1024)(128)(4,1)} %bitcast.193), calls=%async_computation.7 | async-start | bytes 8388608
  228.4 7.1 %slice-start.5 = ((s8[5767168]{0:T(1024)(128)(4,1)}), s8[1572864]{0:T(1024)(128)(4,1)S(1)}, s32[]{:S(2)}) async-start(s8[5767168]{0:T(1024)(128)(4,1)} %bitcast.193), calls=%async_computation.8 | async-start | bytes 3145728
  235.5 7.3 %slice-start = ((s8[8388608]{0:T(1024)(128)(4,1)}), s8[4194304]{0:T(1024)(128)(4,1)S(1)}, s32[]{:S(2)}) async-start(s8[8388608]{0:T(1024)(128)(4,1)} %bitcast.172), calls=%async_computation.3 | async-start | bytes 8388608
  239.2 3.7 %slice-start.1 = ((s8[8388608]{0:T(1024)(128)(4,1)}), s8[4194304]{0:T(1024)(128)(4,1)S(1)}, s32[]{:S(2)}) async-start(s8[8388608]{0:T(1024)(128)(4,1)} %bitcast.172), calls=%async_computation.4 | async-start | bytes 8388608
  239.2 3.7 %copy-start.9 = (bf16[2048,176]{0,1:T(8,128)(2,1)S(1)}, bf16[2048,176]{0,1:T(8,128)(2,1)}, u32[]{:S(2)}) copy-start(bf16[2048,176]{0,1:T(8,128)(2,1)} %param.31) | copy-start | bytes 2162692
  239.2 3.7 %copy-start.10 = (bf16[2048,176]{0,1:T(8,128)(2,1)S(1)}, bf16[2048,176]{0,1:T(8,128)(2,1)}, u32[]{:S(2)}) copy-start(bf16[2048,176]{0,1:T(8,128)(2,1)} %param.30) | copy-start | bytes 2162692
  246.1 1.7 copy-start.11
  259.5 3.4 %copy-start.3 = (bf16[2048,1024]{1,0:T(8,128)(2,1)}, bf16[2048,1024]{1,0:T(8,128)(2,1)S(1)}, u32[]{:S(2)}) copy-start(bf16[2048,1024]{1,0:T(8,128)(2,1)S(1)} %fusion.14) | copy-start | bytes 12582916
  261.3 5.8 %collective-permute-start.14 = (bf16[4,2,128,1024]{3,2,1,0:T(8,128)(2,1)}, bf16[4,2,128,1024]{3,2,1,0:T(8,128)(2,1)}, u32[]{:S(2)}, u32[]{:S(2)}) collective-permute-start(bf16[4,2,128,1024]{3,2,1,0:T(8,128)(2,1)} %dynamic-slice_bitcast_fusion), channel_id=1, source_target_pairs={{0,1},{1,0},{2,3},{3,2},{4,5},{5,4},{6,7},{7,6},{8,9},{9,8},{10,11... | collective-permute-start | bytes 6291464 | tf_op jit(solution)/shard_map/ppermute | solution.py:68
  264.5 2.0 copy-start.1
  264.6 2.5 copy-start.12
  266.7 7.6 %collective-permute-start.6 = (bf16[4,2,128,1024]{3,2,1,0:T(8,128)(2,1)S(1)}, bf16[4,2,128,1024]{3,2,1,0:T(8,128)(2,1)}, u32[]{:S(2)}, u32[]{:S(2)}) collective-permute-start(bf16[4,2,128,1024]{3,2,1,0:T(8,128)(2,1)S(1)} %dynamic-slice_bitcast_fusion.1), channel_id=1, source_target_pairs={{0,1},{1,0},{2,3},{3,2},{4,5},{5,4},{6,7},{7,6},{8,9},{9,8},{10,11... | collective-permute-start | bytes 6291464 | tf_op jit(solution)/shard_map/ppermute | solution.py:68
  270.3 4.1 %copy-start.2 = (bf16[2048,1024]{1,0:T(8,128)(2,1)S(1)}, bf16[2048,1024]{1,0:T(8,128)(2,1)}, u32[]{:S(2)}) copy-start(bf16[2048,1024]{1,0:T(8,128)(2,1)} %copy-done.1) | copy-start | bytes 12582916
  270.9 10.0 %collective-permute-start.15 = (bf16[2,128,512]{2,1,0:T(8,128)(2,1)S(1)}, bf16[2,128,512]{2,1,0:T(8,128)(2,1)S(1)}, u32[]{:S(2)}, u32[]{:S(2)}) collective-permute-start(bf16[2,128,512]{2,1,0:T(8,128)(2,1)S(1)} %fusion.77), channel_id=1, source_target_pairs={{0,4},{1,5},{2,6},{3,7},{4,8},{5,9},{6,10},{7,11},{8,12},{9,13},{1... | collective-permute-start | bytes 786440 | tf_op jit(solution)/shard_map/ppermute | solution.py:80
  272.5 9.2 %collective-permute-start.18 = (bf16[2,128,512]{2,1,0:T(8,128)(2,1)S(1)}, bf16[2,128,512]{2,1,0:T(8,128)(2,1)S(1)}, u32[]{:S(2)}, u32[]{:S(2)}) collective-permute-start(bf16[2,128,512]{2,1,0:T(8,128)(2,1)S(1)} %fusion.78), channel_id=1, source_target_pairs={{0,12},{1,13},{2,14},{3,15},{4,0},{5,1},{6,2},{7,3},{8,4},{9,5},{1... | collective-permute-start | bytes 786440 | tf_op jit(solution)/shard_map/ppermute | solution.py:81
  277.6 10.5 %collective-permute-start.7 = (bf16[2,128,512]{2,1,0:T(8,128)(2,1)S(1)}, bf16[2,128,512]{2,1,0:T(8,128)(2,1)S(1)}, u32[]{:S(2)}, u32[]{:S(2)}) collective-permute-start(bf16[2,128,512]{2,1,0:T(8,128)(2,1)S(1)} %fusion.75), channel_id=1, source_target_pairs={{0,4},{1,5},{2,6},{3,7},{4,8},{5,9},{6,10},{7,11},{8,12},{9,13},{1... | collective-permute-start | bytes 786440 | tf_op jit(solution)/shard_map/ppermute | solution.py:80
  277.9 10.3 %collective-permute-start.10 = (bf16[2,128,512]{2,1,0:T(8,128)(2,1)S(1)}, bf16[2,128,512]{2,1,0:T(8,128)(2,1)S(1)}, u32[]{:S(2)}, u32[]{:S(2)}) collective-permute-start(bf16[2,128,512]{2,1,0:T(8,128)(2,1)S(1)} %fusion.76), channel_id=1, source_target_pairs={{0,12},{1,13},{2,14},{3,15},{4,0},{5,1},{6,2},{7,3},{8,4},{9,5},{1... | collective-permute-start | bytes 786440 | tf_op jit(solution)/shard_map/ppermute | solution.py:81
  281.0 12.7 %collective-permute-start.16 = (bf16[2,128,512]{2,1,0:T(8,128)(2,1)S(1)}, bf16[2,128,512]{2,1,0:T(8,128)(2,1)S(1)}, u32[]{:S(2)}, u32[]{:S(2)}) collective-permute-start(bf16[2,128,512]{2,1,0:T(8,128)(2,1)S(1)} %fusion.64), channel_id=1, source_target_pairs={{0,4},{1,5},{2,6},{3,7},{4,8},{5,9},{6,10},{7,11},{8,12},{9,13},{1... | collective-permute-start | bytes 786440 | tf_op jit(solution)/shard_map/ppermute | solution.py:80
  281.9 12.0 %collective-permute-start.19 = (bf16[2,128,512]{2,1,0:T(8,128)(2,1)S(1)}, bf16[2,128,512]{2,1,0:T(8,128)(2,1)S(1)}, u32[]{:S(2)}, u32[]{:S(2)}) collective-permute-start(bf16[2,128,512]{2,1,0:T(8,128)(2,1)S(1)} %fusion.62), channel_id=1, source_target_pairs={{0,12},{1,13},{2,14},{3,15},{4,0},{5,1},{6,2},{7,3},{8,4},{9,5},{1... | collective-permute-start | bytes 786440 | tf_op jit(solution)/shard_map/ppermute | solution.py:81
  288.2 11.2 %collective-permute-start.8 = (bf16[2,128,512]{2,1,0:T(8,128)(2,1)S(1)}, bf16[2,128,512]{2,1,0:T(8,128)(2,1)S(1)}, u32[]{:S(2)}, u32[]{:S(2)}) collective-permute-start(bf16[2,128,512]{2,1,0:T(8,128)(2,1)S(1)} %fusion.68), channel_id=1, source_target_pairs={{0,4},{1,5},{2,6},{3,7},{4,8},{5,9},{6,10},{7,11},{8,12},{9,13},{1... | collective-permute-start | bytes 786440 | tf_op jit(solution)/shard_map/ppermute | solution.py:80
  288.3 11.1 %collective-permute-start.11 = (bf16[2,128,512]{2,1,0:T(8,128)(2,1)S(1)}, bf16[2,128,512]{2,1,0:T(8,128)(2,1)S(1)}, u32[]{:S(2)}, u32[]{:S(2)}) collective-permute-start(bf16[2,128,512]{2,1,0:T(8,128)(2,1)S(1)} %fusion.66), channel_id=1, source_target_pairs={{0,12},{1,13},{2,14},{3,15},{4,0},{5,1},{6,2},{7,3},{8,4},{9,5},{1... | collective-permute-start | bytes 786440 | tf_op jit(solution)/shard_map/ppermute | solution.py:81
  293.8 11.2 %collective-permute-start.17 = (bf16[2,128,512]{2,1,0:T(8,128)(2,1)S(1)}, bf16[2,128,512]{2,1,0:T(8,128)(2,1)S(1)}, u32[]{:S(2)}, u32[]{:S(2)}) collective-permute-start(bf16[2,128,512]{2,1,0:T(8,128)(2,1)S(1)} %fusion.63), channel_id=1, source_target_pairs={{0,4},{1,5},{2,6},{3,7},{4,8},{5,9},{6,10},{7,11},{8,12},{9,13},{1... | collective-permute-start | bytes 786440 | tf_op jit(solution)/shard_map/ppermute | solution.py:80
  294.0 11.1 %collective-permute-start.20 = (bf16[2,128,512]{2,1,0:T(8,128)(2,1)S(1)}, bf16[2,128,512]{2,1,0:T(8,128)(2,1)S(1)}, u32[]{:S(2)}, u32[]{:S(2)}) collective-permute-start(bf16[2,128,512]{2,1,0:T(8,128)(2,1)S(1)} %fusion.61), channel_id=1, source_target_pairs={{0,12},{1,13},{2,14},{3,15},{4,0},{5,1},{6,2},{7,3},{8,4},{9,5},{1... | collective-permute-start | bytes 786440 | tf_op jit(solution)/shard_map/ppermute | solution.py:81
  299.4 9.9 %collective-permute-start.9 = (bf16[2,128,512]{2,1,0:T(8,128)(2,1)S(1)}, bf16[2,128,512]{2,1,0:T(8,128)(2,1)S(1)}, u32[]{:S(2)}, u32[]{:S(2)}) collective-permute-start(bf16[2,128,512]{2,1,0:T(8,128)(2,1)S(1)} %fusion.67), channel_id=1, source_target_pairs={{0,4},{1,5},{2,6},{3,7},{4,8},{5,9},{6,10},{7,11},{8,12},{9,13},{1... | collective-permute-start | bytes 786440 | tf_op jit(solution)/shard_map/ppermute | solution.py:80
  299.6 12.0 %copy-start.4 = (bf16[2048,128]{1,0:T(8,128)(2,1)S(1)}, bf16[2048,128]{1,0:T(8,128)(2,1)}, u32[]{:S(2)}) copy-start(bf16[2048,128]{1,0:T(8,128)(2,1)} %get-tuple-element.96) | copy-start | bytes 1572868
  299.6 9.7 %collective-permute-start.12 = (bf16[2,128,512]{2,1,0:T(8,128)(2,1)S(1)}, bf16[2,128,512]{2,1,0:T(8,128)(2,1)S(1)}, u32[]{:S(2)}, u32[]{:S(2)}) collective-permute-start(bf16[2,128,512]{2,1,0:T(8,128)(2,1)S(1)} %fusion.65), channel_id=1, source_target_pairs={{0,12},{1,13},{2,14},{3,15},{4,0},{5,1},{6,2},{7,3},{8,4},{9,5},{1... | collective-permute-start | bytes 786440 | tf_op jit(solution)/shard_map/ppermute | solution.py:81
  305.2 12.0 %collective-permute-start.21 = (bf16[128,1024]{1,0:T(8,128)(2,1)S(1)}, bf16[128,1024]{1,0:T(8,128)(2,1)}, u32[]{:S(2)}, u32[]{:S(2)}) collective-permute-start(bf16[128,1024]{1,0:T(8,128)(2,1)S(1)} %fusion.80), channel_id=1, source_target_pairs={{0,2},{1,3},{2,0},{3,1},{4,6},{5,7},{6,4},{7,5},{8,10},{9,11},{10,... | collective-permute-start | bytes 786440 | tf_op jit(solution)/shard_map/ppermute | solution.py:96
  310.2 8.1 %collective-permute-start.13 = (bf16[128,1024]{1,0:T(8,128)(2,1)}, bf16[128,1024]{1,0:T(8,128)(2,1)}, u32[]{:S(2)}, u32[]{:S(2)}) collective-permute-start(bf16[128,1024]{1,0:T(8,128)(2,1)} %fusion.79), channel_id=1, source_target_pairs={{0,2},{1,3},{2,0},{3,1},{4,6},{5,7},{6,4},{7,5},{8,10},{9,11},{10,... | collective-permute-start | bytes 786440 | tf_op jit(solution)/shard_map/ppermute | solution.py:96
Sparse Core Ops, SparseCore 0:
  10.6 85.4 all-gather.2
  163.3 50.8 all-gather.4
